TPU v7x, 256 devices: a whole 4x4x8 slice. The times are simulated.
256 devices in a mesh: cfg: 2 (over core), req: 16 (over x, y), tp: 8 (over z).
Axes of the slice: x: 4, y: 4, z: 8, core: 2. Of those that a mesh axis runs over, the one named last changes fastest.
Arguments:
- latent: float32 [6144, 64], P(('req', 'tp')), may hold values from -6 to 6
- states: float32 [2, 6144, 1536], P('cfg', ('req', 'tp')), may hold values from -12 to 12
- token_counts: int32 [3], replicated, may hold values from 1 to 3840, 6144 in all
- text_lens: int32 [2, 3], P('cfg'), may hold values from 1 to 512, 768 in all within a row
- steps_index: int32 [3], replicated, may hold values from 0 to 49
- modulation: float32 [3, 6, 1536], replicated, may hold values from -3 to 3
- self_qkv: bfloat16 [1536, 3, 2048], P(None, None, 'tp'), may hold values from -0.15625 to 0.15625
- self_out: bfloat16 [2048, 1536], P('tp'), may hold values from -0.15625 to 0.15625
- qk_gains: float32 [4, 2048], P(None, 'tp'), may hold values from 0.8 to 2
- cross_query: bfloat16 [1536, 2048], P(None, 'tp'), may hold values from -1 to 1
- cross_out: bfloat16 [2048, 1536], P('tp'), may hold values from -0.15625 to 0.15625
- cross_gain: float32 [1536], replicated, may hold values from 0.25 to 1.75
- text_kv: bfloat16 [2, 3, 2, 512, 2048], P('cfg', None, None, None, 'tp'), may hold values from -6 to 6
- ffn_in_weight: bfloat16 [8960, 1536], P(('cfg', 'tp')), may hold values from -0.15625 to 0.15625
- ffn_out_weight: bfloat16 [8960, 1536], P(('cfg', 'tp')), may hold values from -0.0625 to 0.0625
- head_weight: bfloat16 [1536, 64], replicated, may hold values from -0.15625 to 0.15625
Outputs:
- new_latent: float32 [6144, 64], P(('req', 'tp'), 'cfg')
- velocity: float32 [6144, 64], P(('req', 'tp'), 'cfg')
- peak: float32 [3], replicated
Inputs may be any that keep to these rules, and one draw needn't show every extreme that they name: `token_counts`: the counts sum to 6144 and the largest is exactly 3840. `text_lens`: in each prompt half the counts sum to 768 and the largest is exactly 512.
All inputs are finite; a program needn't handle non-finite values.
Results may differ from a plain program's by a relative error of at most 0.03.
Values may be sent and summed in bfloat16 or wider, within the bound.
No kernel may reach another device: no remote copies, remote signals or barrier semaphores. Data moves between devices by JAX's collectives and lax.ppermute only.
A program may use at most 64 MiB of HBM per device.

v0:
```python
import jax
import jax.numpy as jnp
from jax import lax
from jax.sharding import PartitionSpec as P

HEADS = 12
HD = 128
STEPS = 50


key_block = 1024
guide_scale = 5.0
rescale_mix = 0.7
flow_shift = 5.0
norm_eps = 1e-06
stat_eps = 1e-05


def swapped(value, axis, stride):
    mask = 2**stride
    pairs = [(source, source ^ mask) for source in range(lax.axis_size(axis))]
    return lax.ppermute(value, axis, pairs)


def layer_norm(values):
    average = jnp.mean(values, axis=-1, keepdims=True)
    centered = values - average
    spread = jnp.mean(centered * centered, axis=-1, keepdims=True)
    return centered * lax.rsqrt(spread + norm_eps)


def rms_scale(values, square_sum, width, gains):
    return (values * lax.rsqrt(square_sum / width + norm_eps)[:, None] * gains).astype(jnp.bfloat16)


def request_of(positions, request_ends):
    return jnp.sum((positions[:, None] >= request_ends[None, :]).astype(jnp.int32), axis=1)


def presence(request_ids, request_count):
    return jnp.any(
        request_ids[:, None] == jnp.arange(request_count, dtype=jnp.int32)[None, :], axis=0
    )


def attend(running, queries, query_req, key_rows, value_rows, key_req, head_count, head_width):
    numerator, denominator = running
    query_count = queries.shape[0]
    key_count = key_rows.shape[0]
    scores = jnp.einsum(
        "qhd,khd->hqk",
        queries.reshape(query_count, head_count, head_width),
        key_rows.reshape(key_count, head_count, head_width),
        preferred_element_type=jnp.float32,
    ) * head_width ** (-0.5)
    same_req = query_req[:, None] == key_req[None, :]
    weights = jnp.where(same_req[None, :, :], jnp.exp(scores), 0.0)
    partial_sum = jnp.einsum(
        "hqk,khd->qhd",
        weights.astype(jnp.bfloat16),
        value_rows.reshape(key_count, head_count, head_width),
        preferred_element_type=jnp.float32,
    )
    return (
        numerator + partial_sum.reshape(query_count, head_count * head_width),
        denominator + jnp.transpose(jnp.sum(weights, axis=2)),
    )


def finish_heads(running, keep_cols, head_count, head_width):
    numerator, denominator = running
    query_count = numerator.shape[0]
    mixed = numerator.reshape(query_count, head_count, head_width) / denominator[:, :, None]
    return (mixed.reshape(query_count, head_count * head_width) * keep_cols).astype(jnp.bfloat16)


def fold_keys(
    running,
    queries,
    query_req,
    key_rows,
    value_rows,
    request_ends,
    all_tokens,
    head_count,
    head_width,
):
    key_total = key_rows.shape[0]
    request_count = request_ends.shape[0]
    wanted = presence(query_req, request_count)

    def visit_block(current, key_part, value_part, part_start):
        part_rows = key_part.shape[0]
        key_pos = part_start + jnp.arange(part_rows, dtype=jnp.int32)
        inside = (key_pos >= 0) & (key_pos < all_tokens)
        key_req = jnp.where(inside, request_of(key_pos, request_ends), -1)
        intersection = jnp.any(wanted & presence(key_req, request_count))

        def compute(state_now):
            return attend(
                state_now, queries, query_req, key_part, value_part, key_req, head_count, head_width
            )

        def skip(state_now):
            return state_now

        return lax.cond(intersection, compute, skip, current)

    full_blocks = key_total // key_block
    key_full = key_rows.reshape(full_blocks, key_block, key_rows.shape[1])
    value_full = value_rows.reshape(full_blocks, key_block, value_rows.shape[1])
    block_starts = key_block * jnp.arange(full_blocks, dtype=jnp.int32)

    def scan_step(current, block_inputs):
        return (visit_block(current, block_inputs[0], block_inputs[1], block_inputs[2]), None)

    running, unused = lax.scan(scan_step, running, (key_full, value_full, block_starts))
    return running


def gather_project(row_block, weight):
    return jnp.dot(
        lax.all_gather(row_block, "tp", axis=0, tiled=True),
        weight,
        preferred_element_type=jnp.float32,
    )


def scatter_project(mixed, weight):
    return lax.psum_scatter(
        jnp.dot(mixed, weight, preferred_element_type=jnp.float32).astype(jnp.bfloat16),
        "tp",
        scatter_dimension=0,
        tiled=True,
    ).astype(jnp.float32)


def feed_forward(ffn_rows, in_weight, out_weight):
    up_part = lax.dot_general(
        lax.all_gather(ffn_rows, ("cfg", "tp"), axis=0, tiled=True),
        in_weight,
        (((1,), (1,)), ((), ())),
        preferred_element_type=jnp.float32,
    )
    activated = jax.nn.gelu(up_part, approximate=True).astype(jnp.bfloat16)
    return lax.psum_scatter(
        jnp.dot(activated, out_weight, preferred_element_type=jnp.float32).astype(jnp.bfloat16),
        ("cfg", "tp"),
        scatter_dimension=0,
        tiled=True,
    ).astype(jnp.float32)


def noise_level(step_value):
    fraction = 1.0 - step_value / STEPS
    return flow_shift * fraction / (1.0 + (flow_shift - 1.0) * fraction)


def shards(
    latent,
    states,
    token_counts,
    text_lens,
    steps_index,
    modulation,
    self_qkv,
    self_out,
    qk_gains,
    cross_query,
    cross_out,
    cross_gain,
    text_kv,
    ffn_in_weight,
    ffn_out_weight,
    head_weight,
):
    row_count = latent.shape[0]
    head_width = HD
    local_cols = self_out.shape[0]
    head_count = local_cols // head_width
    model_width = head_weight.shape[0]
    request_count = token_counts.shape[0]
    tp_parts = lax.axis_size("tp")
    block_rows = row_count * tp_parts
    all_tokens = block_rows * lax.axis_size("req")
    request_ends = jnp.cumsum(token_counts)
    request_range = jnp.arange(request_count, dtype=jnp.int32)
    row_pos = (lax.axis_index("req") * tp_parts + lax.axis_index("tp")) * row_count + jnp.arange(
        row_count, dtype=jnp.int32
    )
    row_onehot = (request_of(row_pos, request_ends)[:, None] == request_range[None, :]).astype(
        jnp.float32
    )
    block_first = lax.axis_index("req") * block_rows
    query_req = request_of(block_first + jnp.arange(block_rows, dtype=jnp.int32), request_ends)
    head_ids = lax.axis_index("tp") * head_count + jnp.arange(head_count, dtype=jnp.int32)
    keep_cols = jnp.repeat((head_ids < HEADS).astype(jnp.float32), head_width)
    hidden_zero = states[0]
    row_mods = jnp.dot(
        row_onehot,
        modulation.reshape(request_count, 6 * model_width),
        precision=lax.Precision.HIGHEST,
    )
    shift_attn = row_mods[:, :model_width]
    scale_attn = row_mods[:, model_width : 2 * model_width]
    gate_attn = row_mods[:, 2 * model_width : 3 * model_width]
    shift_ffn = row_mods[:, 3 * model_width : 4 * model_width]
    scale_ffn = row_mods[:, 4 * model_width : 5 * model_width]
    gate_ffn = row_mods[:, 5 * model_width :]
    normed = (layer_norm(hidden_zero) * (1.0 + scale_attn) + shift_attn).astype(jnp.bfloat16)
    projected = gather_project(normed, self_qkv.reshape(model_width, 3 * local_cols))
    query_raw = projected[:, :local_cols] * keep_cols
    key_raw = projected[:, local_cols : 2 * local_cols] * keep_cols
    query_sq, key_sq = lax.psum(
        (jnp.sum(query_raw * query_raw, axis=1), jnp.sum(key_raw * key_raw, axis=1)), "tp"
    )
    queries = rms_scale(query_raw, query_sq, model_width, qk_gains[0])
    key_rows = rms_scale(key_raw, key_sq, model_width, qk_gains[1])
    value_rows = projected[:, 2 * local_cols :].astype(jnp.bfloat16)
    start_state = (
        jnp.zeros((block_rows, local_cols), jnp.float32),
        jnp.zeros((block_rows, head_count), jnp.float32),
    )
    running = fold_keys(
        start_state,
        queries,
        query_req,
        lax.all_gather(key_rows, "req", axis=0, tiled=True),
        lax.all_gather(value_rows, "req", axis=0, tiled=True),
        request_ends,
        all_tokens,
        head_count,
        head_width,
    )
    self_mix = finish_heads(running, keep_cols, head_count, head_width)
    hidden_one = hidden_zero + gate_attn * scatter_project(self_mix, self_out)
    cross_in = (layer_norm(hidden_one) * cross_gain).astype(jnp.bfloat16)
    cross_raw = gather_project(cross_in, cross_query) * keep_cols
    text_local = text_kv[0]
    text_slots = text_local.shape[2]
    text_raw = (
        text_local[:, 0].reshape(request_count * text_slots, local_cols).astype(jnp.float32)
        * keep_cols
    )
    cross_sq, text_sq = lax.psum(
        (jnp.sum(cross_raw * cross_raw, axis=1), jnp.sum(text_raw * text_raw, axis=1)), "tp"
    )
    cross_q = rms_scale(cross_raw, cross_sq, model_width, qk_gains[2])
    text_keys = rms_scale(text_raw, text_sq, model_width, qk_gains[3])
    text_values = text_local[:, 1].reshape(request_count * text_slots, local_cols)
    text_req = jnp.repeat(request_range, text_slots)
    text_pos = jnp.tile(jnp.arange(text_slots, dtype=jnp.int32), request_count)
    text_limit = jnp.sum(
        jnp.where(text_req[:, None] == request_range[None, :], text_lens[0][None, :], 0), axis=1
    )
    text_req = jnp.where(text_pos < text_limit, text_req, -1)
    cross_state = attend(
        start_state, cross_q, query_req, text_keys, text_values, text_req, head_count, head_width
    )
    cross_mix = finish_heads(cross_state, keep_cols, head_count, head_width)
    hidden_two = hidden_one + scatter_project(cross_mix, cross_out)
    ffn_in = (layer_norm(hidden_two) * (1.0 + scale_ffn) + shift_ffn).astype(jnp.bfloat16)
    hidden_three = hidden_two + gate_ffn * feed_forward(ffn_in, ffn_in_weight, ffn_out_weight)
    velocity_own = jnp.dot(
        layer_norm(hidden_three).astype(jnp.bfloat16),
        head_weight,
        preferred_element_type=jnp.float32,
    )
    velocity_other = swapped(velocity_own, "cfg", 0)
    first_half = lax.axis_index("cfg") == 0
    cond_speed = jnp.where(first_half, velocity_own, velocity_other)
    plain_speed = jnp.where(first_half, velocity_other, velocity_own)
    guided = plain_speed + guide_scale * (cond_speed - plain_speed)
    row_squares = jnp.stack(
        [jnp.sum(cond_speed * cond_speed, axis=1), jnp.sum(guided * guided, axis=1)], axis=1
    )
    square_sums = jnp.dot(jnp.transpose(row_onehot), row_squares, precision=lax.Precision.HIGHEST)
    peak_speed = jnp.max(row_onehot * jnp.max(jnp.abs(guided), axis=1)[:, None], axis=0)
    square_sums = lax.psum(square_sums, ("req", "tp"))
    peak_speed = lax.pmax(peak_speed, ("req", "tp"))
    entry_counts = token_counts.astype(jnp.float32) * guided.shape[1]
    cond_rms = jnp.sqrt(square_sums[:, 0] / entry_counts + stat_eps)
    guided_rms = jnp.sqrt(square_sums[:, 1] / entry_counts + stat_eps)
    factor = rescale_mix * cond_rms / guided_rms + (1.0 - rescale_mix)
    step_value = steps_index.astype(jnp.float32)
    delta_t = noise_level(step_value + 1.0) - noise_level(step_value)
    per_row = jnp.dot(
        row_onehot, jnp.stack([factor, delta_t], axis=1), precision=lax.Precision.HIGHEST
    )
    velocity = per_row[:, 0:1] * guided
    new_latent = latent + per_row[:, 1:2] * velocity
    own_cols = guided.shape[1] // lax.axis_size("cfg")
    col_start = lax.axis_index("cfg") * own_cols
    velocity_part = lax.dynamic_slice_in_dim(velocity, col_start, own_cols, 1)
    latent_part = lax.dynamic_slice_in_dim(new_latent, col_start, own_cols, 1)
    return (latent_part, velocity_part, factor * peak_speed)


def solution(mesh):
    in_specs = (
        P(("req", "tp"), None),
        P("cfg", ("req", "tp"), None),
        P(),
        P("cfg", None),
        P(),
        P(),
        P(None, None, "tp"),
        P("tp", None),
        P(None, "tp"),
        P(None, "tp"),
        P("tp", None),
        P(),
        P("cfg", None, None, None, "tp"),
        P(("cfg", "tp"), None),
        P(("cfg", "tp"), None),
        P(),
    )
    out_specs = (P(("req", "tp"), "cfg"), P(("req", "tp"), "cfg"), P())
    return jax.shard_map(shards, mesh=mesh, in_specs=in_specs, out_specs=out_specs, check_vma=False)
```

profile of v0, /device:TPU:32, one launch (start us, length us, event | category | flops | bytes accessed | tf_op | source)
XLA Modules:
  0.0 1204.7 jit_solution(5381554380162048766)
XLA Ops:
  7.3 1.1 copy.67
  8.4 1.1 reduce_sum.186
  9.5 1.2 multiply_reduce_fusion.7
  10.7 0.8 reduce-window.8
  11.6 0.9 fusion.63
  12.5 1.2 copy-done.1
  13.7 0.8 fusion.47
  14.6 4.3 copy.49
  18.9 36.6 %all-gather.6.cloned.1.call-done = bf16[384,1536]{1,0:T(8,128)(2,1)} async-done(((bf16[48,1536]{1,0:T(8,128)(2,1)}), bf16[384,1536]{1,0:T(8,128)(2,1)}) %all-gather.6.cloned.1.call-update) | async-done | bytes 1179664 | tf_op jit(solution)/shard_map/all_gather | solution.py:123
  55.6 3.1 fusion.85
  58.7 1.0 copy-done.3
  59.9 15.2 %all-reduce.1 = (f32[384]{0:T(512)S(1)}, f32[384]{0:T(512)S(1)}) all-reduce(f32[384]{0:T(512)S(1)} %get-tuple-element.205, f32[384]{0:T(512)S(1)} %get-tuple-element.204), channel_id=1, replica_groups=mesh['cfg'=2,'req'=16,'tp'=8] {'tp'}, use_global_device_ids=true, to_apply=%region_5.6 | all-reduce | flops 768 | bytes 6144 | tf_op jit(solution)/shard_map/psum | solution.py:214
  75.1 1.9 multiply_convert_fusion.2
  77.1 1.7 slice.132
  79.1 51.5 %all-gather.8.cloned.1.call-done = bf16[6144,256]{1,0:T(8,128)(2,1)} async-done(((bf16[384,256]{1,0:T(8,128)(2,1)}), bf16[6144,256]{1,0:T(8,128)(2,1)}) %all-gather.8.cloned.1.call-update) | async-done | bytes 3145744 | tf_op jit(solution)/shard_map/all_gather | solution.py:228
  130.6 4.7 copy.50
  135.3 49.5 %all-gather.10.cloned.1.call-done = bf16[6144,256]{1,0:T(8,128)(2,1)} async-done(((bf16[384,256]{1,0:T(8,128)(2,1)}), bf16[6144,256]{1,0:T(8,128)(2,1)}) %all-gather.10.cloned.1.call-update) | async-done | bytes 3145744 | tf_op jit(solution)/shard_map/all_gather | solution.py:229
  184.7 4.7 copy.51
  189.5 27.8 %while.12 = (s32[]{:T(128)}, f32[384,256]{0,1:T(8,128)S(1)}, f32[384,2]{0,1:T(2,128)S(1)}, s32[6]{0:T(128)S(1)}, s32[3]{0:T(128)S(1)}, /*index=5*/pred[3]{0:T(51...) while((s32[]{:T(128)}, f32[384,256]{0,1:T(8,128)S(1)}, ...), condition=%wide.region_17.18_spmd, body=%wide.region_10.17_spmd.sunk | while | flops 407887872 | bytes 12441360 | solution.py:117
  190.1 0.6 iota_add_fusion.4
  190.8 0.7 and_select_fusion.3
  192.9 3.6 conditional.2
  192.9 1.3 constant_dynamic-slice_fusion
  194.5 1.0 fusion
  195.5 0.9 fusion.2
  197.1 0.6 iota_add_fusion.4
  197.8 0.7 and_select_fusion.3
  199.9 3.6 conditional.2
  199.9 1.3 constant_dynamic-slice_fusion
  201.5 1.0 fusion
  202.5 0.9 fusion.2
  204.1 0.6 iota_add_fusion.4
  204.9 0.7 and_select_fusion.3
  208.3 0.7 and_select_fusion.3
  211.7 0.7 and_select_fusion.3
  215.2 0.7 and_select_fusion.3
  218.1 2.6 convolution_convert_fusion.2
  220.8 44.9 %reduce-scatter.4.cloned.1.call-done = bf16[48,1536]{1,0:T(8,128)(2,1)} async-done(((bf16[384,1536]{1,0:T(8,128)(2,1)}), bf16[48,1536]{1,0:T(8,128)(2,1)}) %reduce-scatter.4.cloned.1.call-update) | async-done | bytes 147472 | tf_op jit(solution)/shard_map/reduce_scatter | solution.py:130
  265.6 1.2 fusion.78
  267.1 0.8 multiply_convert_fusion.5
  267.9 1.4 multiply_reduce_fusion
  269.4 2.7 fusion.80
  272.1 2.9 reshape.254
  275.0 1.1 reshape_reshape_squeeze.3
  276.6 29.0 %all-gather.12.cloned.1.call-done = bf16[384,1536]{1,0:T(8,128)(2,1)} async-done(((bf16[48,1536]{1,0:T(8,128)(2,1)}), bf16[384,1536]{1,0:T(8,128)(2,1)}) %all-gather.12.cloned.1.call-update) | async-done | bytes 1179664 | tf_op jit(solution)/shard_map/all_gather | solution.py:123
  305.6 2.7 multiply_reduce_fusion.1
  308.3 26.7 %all-reduce = (f32[1536]{0:T(1024)S(1)}, f32[384]{0:T(512)S(1)}) all-reduce(f32[1536]{0:T(1024)S(1)} %reduce_sum.195, f32[384]{0:T(512)S(1)} %get-tuple-element.256), channel_id=1, replica_groups=mesh['cfg'=2,'req'=16,'tp'=8] {'tp'}, use_global_device_ids=true, to_apply=%region_25.26 | all-reduce | flops 1920 | bytes 15360 | tf_op jit(solution)/shard_map/psum | solution.py:245
  335.0 3.4 fusion.82
  338.4 1.6 fusion.29
  340.1 1.2 copy.64
  341.2 1.5 convolution_convert_fusion.1
  342.8 40.7 %reduce-scatter.6.cloned.1.call-done = bf16[48,1536]{1,0:T(8,128)(2,1)} async-done(((bf16[384,1536]{1,0:T(8,128)(2,1)}), bf16[48,1536]{1,0:T(8,128)(2,1)}) %reduce-scatter.6.cloned.1.call-update) | async-done | bytes 147472 | tf_op jit(solution)/shard_map/reduce_scatter | solution.py:130
  383.5 1.0 fusion.59
  384.5 1.1 multiply_reduce_fusion.5
  385.7 1.9 fusion.44
  387.6 38.6 %all-gather.14.cloned.1.call-done = bf16[768,1536]{1,0:T(8,128)(2,1)} async-done(((bf16[48,1536]{1,0:T(8,128)(2,1)}), bf16[768,1536]{1,0:T(8,128)(2,1)}) %all-gather.14.cloned.1.call-update) | async-done | bytes 2359312 | tf_op jit(solution)/shard_map/all_gather | solution.py:140
  426.3 7.9 convolution_convert_fusion
  434.2 67.3 %reduce-scatter.8.cloned.1.call-done = bf16[48,1536]{1,0:T(8,128)(2,1)} async-done(((bf16[768,1536]{1,0:T(8,128)(2,1)}), bf16[48,1536]{1,0:T(8,128)(2,1)}) %reduce-scatter.8.cloned.1.call-update) | async-done | bytes 147472 | tf_op jit(solution)/shard_map/reduce_scatter | solution.py:146
  501.6 1.2 fusion.76
  503.4 1.1 collective-permute-done
  505.0 341.7 %psum.39 = f32[3,2]{0,1:T(2,128)S(1)} all-reduce(f32[3,2]{0,1:T(2,128)S(1)} %fusion.62), channel_id=1, replica_groups=mesh['cfg'=2,'req'=16,'tp'=8] {'req','tp'}, use_global_device_ids=true, to_apply=%region_35.36 | all-reduce | flops 6 | bytes 48 | tf_op jit(solution)/shard_map/psum | solution.py:279
  846.7 348.9 %pmax.7 = f32[3]{0:T(128)S(1)} all-reduce(f32[3]{0:T(128)S(1)} %select_reduce_fusion.1), channel_id=1, replica_groups=mesh['cfg'=2,'req'=16,'tp'=8] {'req','tp'}, use_global_device_ids=true, to_apply=%region_38.39 | all-reduce | flops 3 | bytes 24 | tf_op jit(solution)/shard_map/pmax | solution.py:280
  1196.5 0.7 copy.59
  1197.1 0.7 copy.60
  (128 shorter events, 15.8 us)
Async XLA Ops:
  7.2 419.1 %copy-start = (bf16[560,1536]{1,0:T(8,128)(2,1)S(1)}, bf16[560,1536]{1,0:T(8,128)(2,1)}, u32[]{:S(2)}) copy-start(bf16[560,1536]{1,0:T(8,128)(2,1)} %param.34) | copy-start | bytes 5160964
  7.2 6.5 copy-start.2
  7.2 48.4 %all-gather.6.cloned.1.call-start = ((), (), s32[]{:S(2)}) async-start(), calls=%async_computation.3 | async-start | bytes 1327104 | tf_op jit(solution)/shard_map/all_gather | solution.py:123
  12.5 1.2 copy-start.1
  14.5 4.4 copy-start.10
  14.5 116.1 %all-gather.8.cloned.1.call-start = ((), (), s32[]{:S(2)}) async-start(), calls=%async_computation.4 | async-start | bytes 3342336 | tf_op jit(solution)/shard_map/all_gather | solution.py:228
  58.7 1.0 copy-start.3
  77.1 107.7 %all-gather.10.cloned.1.call-start = ((), (), s32[]{:S(2)}) async-start(), calls=%async_computation.5 | async-start | bytes 3342336 | tf_op jit(solution)/shard_map/all_gather | solution.py:229
  78.9 186.8 %reduce-scatter.4.cloned.1.call-start = ((), (), s32[]{:S(2)}) async-start(), calls=%async_computation.6 | async-start | bytes 1327104 | tf_op jit(solution)/shard_map/reduce_scatter | solution.py:130
  220.7 46.4 %copy-start.9 = (f32[1536]{0:T(1024)S(1)}, f32[1536]{0:T(1024)}, u32[]{:S(2)}) copy-start(f32[1536]{0:T(1024)} %param.31) | copy-start | bytes 18436
  220.7 84.8 %all-gather.12.cloned.1.call-start = ((), (), s32[]{:S(2)}) async-start(), calls=%async_computation.7 | async-start | bytes 1327104 | tf_op jit(solution)/shard_map/all_gather | solution.py:123
  267.8 115.6 %reduce-scatter.6.cloned.1.call-start = ((), (), s32[]{:S(2)}) async-start(), calls=%async_computation.8 | async-start | bytes 1327104 | tf_op jit(solution)/shard_map/reduce_scatter | solution.py:130
  272.1 4.0 copy-start.11
  335.0 3.4 copy-start.5
  338.4 2.8 copy-start.6
  342.7 83.5 %all-gather.14.cloned.1.call-start = ((), (), s32[]{:S(2)}) async-start(), calls=%async_computation.9 | async-start | bytes 2506752 | tf_op jit(solution)/shard_map/all_gather | solution.py:140
  387.6 114.0 %reduce-scatter.8.cloned.1.call-start = ((), (), s32[]{:S(2)}) async-start(), calls=%async_computation.10 | async-start | bytes 2506752 | tf_op jit(solution)/shard_map/reduce_scatter | solution.py:146
  434.2 67.4 %copy-start.4 = (bf16[48,1536]{1,0:T(8,128)(2,1)S(1)}, bf16[48,1536]{1,0:T(8,128)(2,1)}, u32[]{:S(2)}) copy-start(bf16[48,1536]{1,0:T(8,128)(2,1)} %reduce-scatter.6.cloned.1.call-done) | copy-start | bytes 442372
  434.2 68.8 %copy-start.7 = (bf16[1536,64]{0,1:T(8,128)(2,1)S(1)}, bf16[1536,64]{0,1:T(8,128)(2,1)}, u32[]{:S(2)}) copy-start(bf16[1536,64]{0,1:T(8,128)(2,1)} %param.35) | copy-start | bytes 589828
  434.2 69.2 %copy-start.13 = (s32[3]{0:T(128)S(1)}, s32[3]{0:T(128)}, u32[]{:S(2)}) copy-start(s32[3]{0:T(128)} %param.24) | copy-start | bytes 40
  434.2 761.4 %copy-start.12 = (s32[3]{0:T(128)S(1)}, s32[3]{0:T(128)}, u32[]{:S(2)}) copy-start(s32[3]{0:T(128)} %param.22) | copy-start | bytes 40
  434.2 762.1 %copy-start.8 = (f32[48,64]{1,0:T(8,128)S(1)}, f32[48,64]{1,0:T(8,128)}, u32[]{:S(2)}) copy-start(f32[48,64]{1,0:T(8,128)} %param.20) | copy-start | bytes 36868
  503.3 1.3 collective-permute-start
Sparse Core Ops, SparseCore 0:
  14.6 40.8 all-gather.5
  77.2 53.3 all-gather.7
  133.1 51.5 all-gather.9
  220.8 44.7 reduce-scatter.3
  268.0 37.5 all-gather.11
  342.9 40.5 reduce-scatter.5
  387.7 38.5 all-gather.13
  434.4 67.1 reduce-scatter.7
where the time goes:
time: 1210 us; the launch traced here: 1200 us
  blocking collectives  733 us (61%)
  waiting for transfers between devices  359 us (30%)
  other arithmetic  33.2 us (3%)
  local copies, waits for them, and re-layouts  32.2 us (3%)
  matrix products  28.1 us (2%)
  between operations  14.5 us (1%)
    pmax x1, blocking collectives, shards(): peak_speed = lax.pmax(peak_speed, ('req', 'tp'))  349 us
    psum x1, blocking collectives, shards(): square_sums = lax.psum(square_sums, ('req', 'tp'))  342 us
    reduce_scatter x2, waiting for transfers between devices, scatter_project(): lax.psum_scatter(jnp.dot(mixed, weight, preferred_element_type=jnp.float3...  85.6 us
    reduce_scatter x1, waiting for transfers between devices, feed_forward(): lax.psum_scatter(jnp.dot(activated, out_weight, preferred_element_type=jn...  67.3 us
    all_gather x2, waiting for transfers between devices, gather_project(): lax.all_gather(row_block, 'tp', axis=0, tiled=True)  65.6 us
    all_gather x1, waiting for transfers between devices, shards(): lax.all_gather(key_rows, 'req', axis=0, tiled=True)  51.5 us
    all_gather x1, waiting for transfers between devices, shards(): lax.all_gather(value_rows, 'req', axis=0, tiled=True)  49.5 us
    all_gather x1, waiting for transfers between devices, feed_forward(): lax.all_gather(ffn_rows, ('cfg', 'tp'), axis=0, tiled=True)  38.6 us
  transfers between devices with their start and end apart: 9, of which 9 were waited for; matrix products, arithmetic and copies ran while one was open for 2% of the time, Pallas kernels for 0%

commit v1 on v0

--- a/solution.py
+++ b/solution.py
@@ -196,6 +196,12 @@
     head_ids = lax.axis_index("tp") * head_count + jnp.arange(head_count, dtype=jnp.int32)
     keep_cols = jnp.repeat((head_ids < HEADS).astype(jnp.float32), head_width)
     hidden_zero = states[0]
+    text_local = text_kv[0]
+    text_slots = text_local.shape[2]
+    text_raw = (
+        text_local[:, 0].reshape(request_count * text_slots, local_cols).astype(jnp.float32)
+        * keep_cols
+    )
     row_mods = jnp.dot(
         row_onehot,
         modulation.reshape(request_count, 6 * model_width),
@@ -211,12 +217,22 @@
     projected = gather_project(normed, self_qkv.reshape(model_width, 3 * local_cols))
     query_raw = projected[:, :local_cols] * keep_cols
     key_raw = projected[:, local_cols : 2 * local_cols] * keep_cols
-    query_sq, key_sq = lax.psum(
-        (jnp.sum(query_raw * query_raw, axis=1), jnp.sum(key_raw * key_raw, axis=1)), "tp"
+    query_sq, key_sq, text_sq = lax.psum(
+        (
+            jnp.sum(query_raw * query_raw, axis=1),
+            jnp.sum(key_raw * key_raw, axis=1),
+            jnp.sum(text_raw * text_raw, axis=1),
+        ),
+        "tp",
     )
     queries = rms_scale(query_raw, query_sq, model_width, qk_gains[0])
     key_rows = rms_scale(key_raw, key_sq, model_width, qk_gains[1])
     value_rows = projected[:, 2 * local_cols :].astype(jnp.bfloat16)
+    kv_all = lax.all_gather(
+        jnp.concatenate([key_rows, value_rows], axis=1), "req", axis=0, tiled=True
+    )
+    key_all = kv_all[:, :local_cols]
+    value_all = kv_all[:, local_cols:]
     start_state = (
         jnp.zeros((block_rows, local_cols), jnp.float32),
         jnp.zeros((block_rows, head_count), jnp.float32),
@@ -225,8 +241,8 @@
         start_state,
         queries,
         query_req,
-        lax.all_gather(key_rows, "req", axis=0, tiled=True),
-        lax.all_gather(value_rows, "req", axis=0, tiled=True),
+        key_all,
+        value_all,
         request_ends,
         all_tokens,
         head_count,
@@ -236,15 +252,7 @@
     hidden_one = hidden_zero + gate_attn * scatter_project(self_mix, self_out)
     cross_in = (layer_norm(hidden_one) * cross_gain).astype(jnp.bfloat16)
     cross_raw = gather_project(cross_in, cross_query) * keep_cols
-    text_local = text_kv[0]
-    text_slots = text_local.shape[2]
-    text_raw = (
-        text_local[:, 0].reshape(request_count * text_slots, local_cols).astype(jnp.float32)
-        * keep_cols
-    )
-    cross_sq, text_sq = lax.psum(
-        (jnp.sum(cross_raw * cross_raw, axis=1), jnp.sum(text_raw * text_raw, axis=1)), "tp"
-    )
+    cross_sq = lax.psum(jnp.sum(cross_raw * cross_raw, axis=1), "tp")
     cross_q = rms_scale(cross_raw, cross_sq, model_width, qk_gains[2])
     text_keys = rms_scale(text_raw, text_sq, model_width, qk_gains[3])
     text_values = text_local[:, 1].reshape(request_count * text_slots, local_cols)
@@ -276,8 +284,15 @@
     )
     square_sums = jnp.dot(jnp.transpose(row_onehot), row_squares, precision=lax.Precision.HIGHEST)
     peak_speed = jnp.max(row_onehot * jnp.max(jnp.abs(guided), axis=1)[:, None], axis=0)
-    square_sums = lax.psum(square_sums, ("req", "tp"))
-    peak_speed = lax.pmax(peak_speed, ("req", "tp"))
+    slot_count = lax.axis_size("req") * tp_parts
+    slot = lax.axis_index("req") * tp_parts + lax.axis_index("tp")
+    peak_slots = jnp.where(
+        (jnp.arange(slot_count, dtype=jnp.int32) == slot)[:, None], peak_speed[None, :], 0.0
+    )
+    packed = jnp.concatenate([square_sums.reshape(-1), peak_slots.reshape(-1)])
+    packed = lax.psum(jnp.where(lax.axis_index("cfg") == 0, packed, 0.0), ("cfg", "req", "tp"))
+    square_sums = packed[: 2 * request_count].reshape(request_count, 2)
+    peak_speed = jnp.max(packed[2 * request_count :].reshape(slot_count, request_count), axis=0)
     entry_counts = token_counts.astype(jnp.float32) * guided.shape[1]
     cond_rms = jnp.sqrt(square_sums[:, 0] / entry_counts + stat_eps)
     guided_rms = jnp.sqrt(square_sums[:, 1] / entry_counts + stat_eps)

time: 1210 us -> 566 us (0.47)
  the two profiles are of different devices: /device:TPU:32 before, /device:TPU:2 now
where the time goes in v1:
time: 566 us; the launch traced here: 562 us
  waiting for transfers between devices  319 us (56%)
  blocking collectives  121 us (21%)
  local copies, waits for them, and re-layouts  39.2 us (7%)
  other arithmetic  33.9 us (6%)
  matrix products  30 us (5%)
  between operations  14.5 us (3%)
    reduce_scatter x2, waiting for transfers between devices, scatter_project(): lax.psum_scatter(jnp.dot(mixed, weight, preferred_element_type=jnp.float3...  82 us
    psum x1, blocking collectives, shards(): lax.psum(jnp.where(lax.axis_index('cfg') == 0, packed, 0.0), ('cfg', 'req...  76.9 us
    all_gather x2, waiting for transfers between devices, gather_project(): lax.all_gather(row_block, 'tp', axis=0, tiled=True)  66.5 us
    all_gather x1, waiting for transfers between devices, shards(): lax.all_gather(jnp.concatenate([key_rows, value_rows], axis=1), 'req', ax...  65.8 us
    reduce_scatter x1, waiting for transfers between devices, feed_forward(): lax.psum_scatter(jnp.dot(activated, out_weight, preferred_element_type=jn...  64.9 us
    psum x2, blocking collectives, shards(): lax.psum((jnp.sum(query_raw * query_raw, axis=1), jnp.sum(key_raw * key_r...  43.8 us
    all_gather x1, waiting for transfers between devices, feed_forward(): lax.all_gather(ffn_rows, ('cfg', 'tp'), axis=0, tiled=True)  38.5 us
  transfers between devices with their start and end apart: 8, of which 8 were waited for; matrix products, arithmetic and copies ran while one was open for 2% of the time, Pallas kernels for 0%

profile of v1, /device:TPU:2, one launch (start us, length us, event | category | flops | bytes accessed | tf_op | source)
XLA Modules:
  0.0 562.2 jit_solution(6461795953916605860)
XLA Ops:
  7.3 1.1 copy.71
  8.4 1.1 reduce_sum.186
  9.5 1.2 multiply_reduce_fusion.7
  10.7 0.8 reduce-window.8
  11.6 0.9 fusion.63
  12.5 1.2 copy-done.1
  13.7 0.8 fusion.47
  14.6 4.3 copy.51
  19.0 37.5 %all-gather.5.cloned.1.call-done = bf16[384,1536]{1,0:T(8,128)(2,1)} async-done(((bf16[48,1536]{1,0:T(8,128)(2,1)}), bf16[384,1536]{1,0:T(8,128)(2,1)}) %all-gather.5.cloned.1.call-update) | async-done | bytes 1179664 | tf_op jit(solution)/shard_map/all_gather | solution.py:123
  56.5 3.1 fusion.88
  59.7 1.0 copy-done.3
  60.8 15.5 %all-reduce.1 = (f32[384]{0:T(512)S(1)}, f32[384]{0:T(512)S(1)}) all-reduce(f32[384]{0:T(512)S(1)} %get-tuple-element.205, f32[384]{0:T(512)S(1)} %get-tuple-element.204), channel_id=1, replica_groups=mesh['cfg'=2,'req'=16,'tp'=8] {'tp'}, use_global_device_ids=true, to_apply=%region_5.6 | all-reduce | flops 768 | bytes 6144 | tf_op jit(solution)/shard_map/psum | solution.py:220
  76.4 1.3 multiply_convert_fusion.2
  77.7 0.8 pad_maximum_fusion
  78.8 65.8 %all-gather.7.cloned.1.call-done = bf16[6144,512]{1,0:T(8,128)(2,1)} async-done(((bf16[384,512]{1,0:T(8,128)(2,1)}), bf16[6144,512]{1,0:T(8,128)(2,1)}) %all-gather.7.cloned.1.call-update) | async-done | bytes 6291472 | tf_op jit(solution)/shard_map/all_gather | solution.py:231
  144.6 5.9 %fusion.82 = (bf16[6144,256]{1,0:T(8,128)(2,1)}, bf16[6144,256]{1,0:T(8,128)(2,1)}) fusion(bf16[6144,512]{1,0:T(8,128)(2,1)} %all-gather.7.cloned.1.call-done), kind=kLoop, calls=%fused_computation.164 | loop fusion | bytes 12582912 | tf_op jit(solution)/shard_map/slice | solution.py:235
  150.5 4.7 copy.52
  155.2 4.7 copy.53
  159.9 31.4 %while.12 = (s32[]{:T(128)}, f32[384,256]{0,1:T(8,128)S(1)}, f32[384,2]{0,1:T(2,128)S(1)}, s32[6]{0:T(128)S(1)}, s32[3]{0:T(128)S(1)}, /*index=5*/pred[3]{0:T(51...) while((s32[]{:T(128)}, f32[384,256]{0,1:T(8,128)S(1)}, ...), condition=%wide.region_17.18_spmd, body=%wide.region_10.17_spmd.sunk | while | flops 407887872 | bytes 12441360 | solution.py:117
  161.3 0.7 and_select_fusion.3
  163.4 3.6 conditional.2
  163.4 1.3 constant_dynamic-slice_fusion
  164.9 1.0 fusion
  166.0 0.9 fusion.2
  168.3 0.7 and_select_fusion.3
  170.4 3.6 conditional.2
  170.4 1.3 constant_dynamic-slice_fusion
  172.0 1.0 fusion
  173.0 0.9 fusion.2
  175.3 0.7 and_select_fusion.3
  177.4 3.6 conditional.2
  177.4 1.3 constant_dynamic-slice_fusion
  179.0 1.0 fusion
  180.1 0.9 fusion.2
  182.4 0.7 and_select_fusion.3
  185.8 0.7 and_select_fusion.3
  189.3 0.7 and_select_fusion.3
  192.1 2.6 convolution_convert_fusion.2
  194.8 42.8 %reduce-scatter.4.cloned.1.call-done = bf16[48,1536]{1,0:T(8,128)(2,1)} async-done(((bf16[384,1536]{1,0:T(8,128)(2,1)}), bf16[48,1536]{1,0:T(8,128)(2,1)}) %reduce-scatter.4.cloned.1.call-update) | async-done | bytes 147472 | tf_op jit(solution)/shard_map/reduce_scatter | solution.py:130
  237.7 1.2 fusion.80
  239.1 0.8 multiply_convert_fusion.5
  239.9 1.4 multiply_reduce_fusion
  241.4 2.7 fusion.83
  244.1 2.9 reshape.292
  247.0 1.1 reshape_reshape_squeeze.3
  248.6 29.0 %all-gather.9.cloned.1.call-done = bf16[384,1536]{1,0:T(8,128)(2,1)} async-done(((bf16[48,1536]{1,0:T(8,128)(2,1)}), bf16[384,1536]{1,0:T(8,128)(2,1)}) %all-gather.9.cloned.1.call-update) | async-done | bytes 1179664 | tf_op jit(solution)/shard_map/all_gather | solution.py:123
  277.6 2.7 multiply_reduce_fusion.1
  280.3 28.3 %all-reduce = (f32[1536]{0:T(1024)S(1)}, f32[384]{0:T(512)S(1)}) all-reduce(f32[1536]{0:T(1024)S(1)} %reduce_sum.195, f32[384]{0:T(512)S(1)} %get-tuple-element.260), channel_id=1, replica_groups=mesh['cfg'=2,'req'=16,'tp'=8] {'tp'}, use_global_device_ids=true, to_apply=%region_25.26 | all-reduce | flops 1920 | bytes 15360 | tf_op jit(solution)/shard_map/psum | solution.py:220
  308.6 3.4 fusion.85
  312.0 1.6 fusion.29
  313.6 1.2 copy.68
  314.8 1.5 convolution_convert_fusion.1
  316.4 39.2 %reduce-scatter.6.cloned.1.call-done = bf16[48,1536]{1,0:T(8,128)(2,1)} async-done(((bf16[384,1536]{1,0:T(8,128)(2,1)}), bf16[48,1536]{1,0:T(8,128)(2,1)}) %reduce-scatter.6.cloned.1.call-update) | async-done | bytes 147472 | tf_op jit(solution)/shard_map/reduce_scatter | solution.py:130
  355.6 1.0 fusion.59
  356.6 1.1 multiply_reduce_fusion.5
  357.7 1.9 fusion.44
  359.7 38.5 %all-gather.11.cloned.1.call-done = bf16[768,1536]{1,0:T(8,128)(2,1)} async-done(((bf16[48,1536]{1,0:T(8,128)(2,1)}), bf16[768,1536]{1,0:T(8,128)(2,1)}) %all-gather.11.cloned.1.call-update) | async-done | bytes 2359312 | tf_op jit(solution)/shard_map/all_gather | solution.py:140
  398.3 7.9 %convolution_convert_fusion = bf16[768,1536]{1,0:T(8,128)(2,1)} fusion(bf16[560,1536]{1,0:T(8,128)(2,1)S(1)} %copy-done, bf16[768,1536]{1,0:T(8,128)(2,1)} %all-gather.11.cloned.1.call-done, bf16[560,1536]{1,0:T(8,128)(2,1)} %param.33), kind=kOutput, calls=%fused_computation.25 | convolution fusion | flops 2647461888 | bytes 8159232 | tf_op jit(solution)/shard_map/dot_general | solution.py:147
  406.9 64.9 %reduce-scatter.8.cloned.1.call-done = bf16[48,1536]{1,0:T(8,128)(2,1)} async-done(((bf16[768,1536]{1,0:T(8,128)(2,1)}), bf16[48,1536]{1,0:T(8,128)(2,1)}) %reduce-scatter.8.cloned.1.call-update) | async-done | bytes 147472 | tf_op jit(solution)/shard_map/reduce_scatter | solution.py:146
  471.8 1.2 fusion.78
  473.6 1.1 collective-permute-done
  475.7 76.9 %psum.39 = f32[390]{0:T(512)S(1)} all-reduce(f32[390]{0:T(512)S(1)} %maximum_select_fusion), channel_id=1, replica_groups=mesh['cfg'=2,'req'=16,'tp'=8] {'cfg','req','tp'}, use_global_device_ids=true, to_apply=%region_37.38 | all-reduce | flops 390 | bytes 3120 | tf_op jit(solution)/shard_map/psum | solution.py:293
  553.9 0.7 copy.62
  554.6 0.7 copy.63
  (144 shorter events, 19.7 us)
Async XLA Ops:
  7.2 391.1 %copy-start = (bf16[560,1536]{1,0:T(8,128)(2,1)S(1)}, bf16[560,1536]{1,0:T(8,128)(2,1)}, u32[]{:S(2)}) copy-start(bf16[560,1536]{1,0:T(8,128)(2,1)} %param.34) | copy-start | bytes 5160964
  7.2 6.6 %copy-start.2 = (f32[1,48,1536]{2,1,0:T(8,128)S(1)}, f32[1,48,1536]{2,1,0:T(8,128)}, u32[]{:S(2)}) copy-start(f32[1,48,1536]{2,1,0:T(8,128)} %param.21) | copy-start | bytes 884740
  7.2 49.3 %all-gather.5.cloned.1.call-start = ((), (), s32[]{:S(2)}) async-start(), calls=%async_computation.3 | async-start | bytes 1327104 | tf_op jit(solution)/shard_map/all_gather | solution.py:123
  12.5 1.2 copy-start.1
  14.5 4.4 copy-start.10
  14.6 130.1 %all-gather.7.cloned.1.call-start = ((), (), s32[]{:S(2)}) async-start(), calls=%async_computation.4 | async-start | bytes 6684672 | tf_op jit(solution)/shard_map/all_gather | solution.py:231
  59.6 1.0 copy-start.3
  78.5 159.1 %reduce-scatter.4.cloned.1.call-start = ((), (), s32[]{:S(2)}) async-start(), calls=%async_computation.5 | async-start | bytes 1327104 | tf_op jit(solution)/shard_map/reduce_scatter | solution.py:130
  194.8 44.3 %copy-start.9 = (f32[1536]{0:T(1024)S(1)}, f32[1536]{0:T(1024)}, u32[]{:S(2)}) copy-start(f32[1536]{0:T(1024)} %param.31) | copy-start | bytes 18436
  194.8 82.8 %all-gather.9.cloned.1.call-start = ((), (), s32[]{:S(2)}) async-start(), calls=%async_computation.6 | async-start | bytes 1327104 | tf_op jit(solution)/shard_map/all_gather | solution.py:123
  239.9 115.7 %reduce-scatter.6.cloned.1.call-start = ((), (), s32[]{:S(2)}) async-start(), calls=%async_computation.7 | async-start | bytes 1327104 | tf_op jit(solution)/shard_map/reduce_scatter | solution.py:130
  244.1 4.0 copy-start.11
  308.6 3.4 copy-start.5
  312.0 2.8 copy-start.6
  316.3 81.9 %all-gather.11.cloned.1.call-start = ((), (), s32[]{:S(2)}) async-start(), calls=%async_computation.8 | async-start | bytes 2506752 | tf_op jit(solution)/shard_map/all_gather | solution.py:140
  359.7 112.1 %reduce-scatter.8.cloned.1.call-start = ((), (), s32[]{:S(2)}) async-start(), calls=%async_computation.9 | async-start | bytes 2506752 | tf_op jit(solution)/shard_map/reduce_scatter | solution.py:146
  406.2 0.7 copy-start.13
  406.2 65.6 %copy-start.4 = (bf16[48,1536]{1,0:T(8,128)(2,1)S(1)}, bf16[48,1536]{1,0:T(8,128)(2,1)}, u32[]{:S(2)}) copy-start(bf16[48,1536]{1,0:T(8,128)(2,1)} %reduce-scatter.6.cloned.1.call-done) | copy-start | bytes 442372
  406.2 67.0 %copy-start.7 = (bf16[1536,64]{0,1:T(8,128)(2,1)S(1)}, bf16[1536,64]{0,1:T(8,128)(2,1)}, u32[]{:S(2)}) copy-start(bf16[1536,64]{0,1:T(8,128)(2,1)} %param.35) | copy-start | bytes 589828
  406.8 146.2 %copy-start.12 = (s32[3]{0:T(128)S(1)}, s32[3]{0:T(128)}, u32[]{:S(2)}) copy-start(s32[3]{0:T(128)} %param.22) | copy-start | bytes 40
  406.8 147.0 %copy-start.8 = (f32[48,64]{1,0:T(8,128)S(1)}, f32[48,64]{1,0:T(8,128)}, u32[]{:S(2)}) copy-start(f32[48,64]{1,0:T(8,128)} %param.20) | copy-start | bytes 36868
  473.5 1.3 collective-permute-start
Sparse Core Ops, SparseCore 0:
  14.7 41.7 all-gather.4
  78.6 65.9 all-gather.6
  194.9 42.7 reduce-scatter.3
  240.0 37.5 all-gather.8
  316.5 39.0 reduce-scatter.5
  359.8 38.4 all-gather.10
  406.3 65.4 reduce-scatter.7

commit v2 on v1

--- a/solution.py
+++ b/solution.py
@@ -20,6 +20,47 @@
     mask = 2**stride
     pairs = [(source, source ^ mask) for source in range(lax.axis_size(axis))]
     return lax.ppermute(value, axis, pairs)
+
+
+def shifted(value, axis, step):
+    size = lax.axis_size(axis)
+    return lax.ppermute(value, axis, [(source, (source + step) % size) for source in range(size)])
+
+
+def ring_gather(value, axis):
+    size = lax.axis_size(axis)
+    forward, backward = value, value
+    ahead, behind = [], []
+    for unused in range(size // 2):
+        forward = shifted(forward, axis, 1)
+        behind.append(forward)
+    for unused in range((size - 1) // 2):
+        backward = shifted(backward, axis, -1)
+        ahead.append(backward)
+    by_offset = jnp.stack([value] + ahead + behind[::-1])
+    doubled = jnp.concatenate([by_offset, by_offset], axis=0)
+    start = (size - lax.axis_index(axis)) % size
+    ordered = lax.dynamic_slice_in_dim(doubled, start, size, axis=0)
+    return ordered.reshape((size * value.shape[0],) + value.shape[1:])
+
+
+def scatter_sum(value, axis):
+    size = lax.axis_size(axis)
+    me = lax.axis_index(axis)
+    blocks = value.reshape((size, value.shape[0] // size) + value.shape[1:])
+    total = lax.dynamic_index_in_dim(blocks, me, 0, keepdims=False).astype(jnp.float32)
+    for step in range(1, size):
+        outgoing = lax.dynamic_index_in_dim(blocks, (me + step) % size, 0, keepdims=False)
+        total = total + shifted(outgoing, axis, step).astype(jnp.float32)
+    return total
+
+
+def butterfly_sum(value, axis):
+    stride = 1
+    while stride < lax.axis_size(axis):
+        value = value + swapped(value, axis, stride.bit_length() - 1)
+        stride *= 2
+    return value
 
 
 def layer_norm(values):
@@ -119,36 +160,32 @@
 
 
 def gather_project(row_block, weight):
-    return jnp.dot(
-        lax.all_gather(row_block, "tp", axis=0, tiled=True),
-        weight,
-        preferred_element_type=jnp.float32,
-    )
+    return jnp.dot(ring_gather(row_block, "tp"), weight, preferred_element_type=jnp.float32)
 
 
 def scatter_project(mixed, weight):
-    return lax.psum_scatter(
-        jnp.dot(mixed, weight, preferred_element_type=jnp.float32).astype(jnp.bfloat16),
-        "tp",
-        scatter_dimension=0,
-        tiled=True,
-    ).astype(jnp.float32)
+    return scatter_sum(
+        jnp.dot(mixed, weight, preferred_element_type=jnp.float32).astype(jnp.bfloat16), "tp"
+    )
 
 
 def feed_forward(ffn_rows, in_weight, out_weight):
+    partner_in, partner_out = swapped((in_weight, out_weight), "cfg", 0)
+    units = in_weight.shape[0]
+    rows = ring_gather(ffn_rows, "tp")
     up_part = lax.dot_general(
-        lax.all_gather(ffn_rows, ("cfg", "tp"), axis=0, tiled=True),
-        in_weight,
+        rows,
+        jnp.concatenate([in_weight, partner_in], axis=0),
         (((1,), (1,)), ((), ())),
         preferred_element_type=jnp.float32,
     )
     activated = jax.nn.gelu(up_part, approximate=True).astype(jnp.bfloat16)
-    return lax.psum_scatter(
-        jnp.dot(activated, out_weight, preferred_element_type=jnp.float32).astype(jnp.bfloat16),
-        ("cfg", "tp"),
-        scatter_dimension=0,
-        tiled=True,
+    own_term = jnp.dot(activated[:, :units], out_weight, preferred_element_type=jnp.float32)
+    partner_term = jnp.dot(activated[:, units:], partner_out, preferred_element_type=jnp.float32)
+    pair = own_term.astype(jnp.bfloat16).astype(jnp.float32) + partner_term.astype(
+        jnp.bfloat16
     ).astype(jnp.float32)
+    return scatter_sum(pair.astype(jnp.bfloat16), "tp")
 
 
 def noise_level(step_value):
@@ -202,6 +239,7 @@
         text_local[:, 0].reshape(request_count * text_slots, local_cols).astype(jnp.float32)
         * keep_cols
     )
+    text_sq = butterfly_sum(jnp.sum(text_raw * text_raw, axis=1), "tp")
     row_mods = jnp.dot(
         row_onehot,
         modulation.reshape(request_count, 6 * model_width),
@@ -217,14 +255,8 @@
     projected = gather_project(normed, self_qkv.reshape(model_width, 3 * local_cols))
     query_raw = projected[:, :local_cols] * keep_cols
     key_raw = projected[:, local_cols : 2 * local_cols] * keep_cols
-    query_sq, key_sq, text_sq = lax.psum(
-        (
-            jnp.sum(query_raw * query_raw, axis=1),
-            jnp.sum(key_raw * key_raw, axis=1),
-            jnp.sum(text_raw * text_raw, axis=1),
-        ),
-        "tp",
-    )
+    query_sq = butterfly_sum(jnp.sum(query_raw * query_raw, axis=1), "tp")
+    key_sq = butterfly_sum(jnp.sum(key_raw * key_raw, axis=1), "tp")
     queries = rms_scale(query_raw, query_sq, model_width, qk_gains[0])
     key_rows = rms_scale(key_raw, key_sq, model_width, qk_gains[1])
     value_rows = projected[:, 2 * local_cols :].astype(jnp.bfloat16)
@@ -252,7 +284,7 @@
     hidden_one = hidden_zero + gate_attn * scatter_project(self_mix, self_out)
     cross_in = (layer_norm(hidden_one) * cross_gain).astype(jnp.bfloat16)
     cross_raw = gather_project(cross_in, cross_query) * keep_cols
-    cross_sq = lax.psum(jnp.sum(cross_raw * cross_raw, axis=1), "tp")
+    cross_sq = butterfly_sum(jnp.sum(cross_raw * cross_raw, axis=1), "tp")
     cross_q = rms_scale(cross_raw, cross_sq, model_width, qk_gains[2])
     text_keys = rms_scale(text_raw, text_sq, model_width, qk_gains[3])
     text_values = text_local[:, 1].reshape(request_count * text_slots, local_cols)
@@ -284,15 +316,18 @@
     )
     square_sums = jnp.dot(jnp.transpose(row_onehot), row_squares, precision=lax.Precision.HIGHEST)
     peak_speed = jnp.max(row_onehot * jnp.max(jnp.abs(guided), axis=1)[:, None], axis=0)
-    slot_count = lax.axis_size("req") * tp_parts
-    slot = lax.axis_index("req") * tp_parts + lax.axis_index("tp")
-    peak_slots = jnp.where(
-        (jnp.arange(slot_count, dtype=jnp.int32) == slot)[:, None], peak_speed[None, :], 0.0
-    )
-    packed = jnp.concatenate([square_sums.reshape(-1), peak_slots.reshape(-1)])
-    packed = lax.psum(jnp.where(lax.axis_index("cfg") == 0, packed, 0.0), ("cfg", "req", "tp"))
-    square_sums = packed[: 2 * request_count].reshape(request_count, 2)
-    peak_speed = jnp.max(packed[2 * request_count :].reshape(slot_count, request_count), axis=0)
+    packed = jnp.concatenate([square_sums.reshape(-1), peak_speed])
+    sum_count = 2 * request_count
+    for axis in ("tp", "req"):
+        stride = 1
+        while stride < lax.axis_size(axis):
+            other = swapped(packed, axis, stride.bit_length() - 1)
+            packed = jnp.concatenate(
+                [packed[:sum_count] + other[:sum_count], jnp.maximum(packed[sum_count:], other[sum_count:])]
+            )
+            stride *= 2
+    square_sums = packed[:sum_count].reshape(request_count, 2)
+    peak_speed = packed[sum_count:]
     entry_counts = token_counts.astype(jnp.float32) * guided.shape[1]
     cond_rms = jnp.sqrt(square_sums[:, 0] / entry_counts + stat_eps)
     guided_rms = jnp.sqrt(square_sums[:, 1] / entry_counts + stat_eps)

time: 566 us -> 443 us (0.78)
  waiting for transfers between devices: 319 us -> 196 us
  starting transfers between devices: 0.43 us -> 123 us
  blocking collectives: 121 us -> 0 us
  local copies, waits for them, and re-layouts: 39.2 us -> 52.6 us
  matrix products: 30 us -> 20.2 us
  other arithmetic: 33.9 us -> 24.9 us
    reduce_scatter x3 -> x0, waiting for transfers between devices: 147 us -> none  [the longest x2 82 us: scatter_project(): lax.psum_scatter(jnp.dot(mixed, weight, preferred_element_type=jnp.float3...]
    psum x3 -> x0, blocking collectives: 121 us -> none  [the longest x1 76.9 us: shards(): lax.psum(jnp.where(lax.axis_index('cfg') == 0, packed, 0.0), ('cfg', 'req...]
    all_gather x3 -> x0, waiting for transfers between devices: 105 us -> none  [the longest x2 66.5 us: gather_project(): lax.all_gather(row_block, 'tp', axis=0, tiled=True)]
    ppermute x0 -> x42, waiting for transfers between devices: none -> 92.1 us  [shifted(): lax.ppermute(value, axis, [(source, (source + step) % size) for source in...]
    ppermute x0 -> x42, starting transfers between devices: none -> 76.4 us  [shifted(): lax.ppermute(value, axis, [(source, (source + step) % size) for source in...]
    ppermute x1 -> x22, starting transfers between devices: 0.14 us -> 46.7 us  [swapped(): return lax.ppermute(value, axis, pairs)]
    ppermute x1 -> x22, waiting for transfers between devices: 1.13 us -> 37.6 us  [swapped(): return lax.ppermute(value, axis, pairs)]
    unnamed x32 -> x90, local copies, waits for them, and re-layouts: 9.65 us -> 18.4 us
  transfers between devices with their start and end apart: 8 -> 65, of which waited for: 8 -> 46; matrix products, arithmetic and copies ran while one was open for 2% -> 5% of each run, Pallas kernels for 0% -> 0%
where the time goes in v2:
time: 443 us; the launch traced here: 436 us
  waiting for transfers between devices  196 us (44%)
  starting transfers between devices  123 us (28%)
  local copies, waits for them, and re-layouts  52.6 us (12%)
  other arithmetic  24.9 us (6%)
  matrix products  20.2 us (5%)
  between operations  15.5 us (3%)
    ppermute x42, waiting for transfers between devices, shifted(): lax.ppermute(value, axis, [(source, (source + step) % size) for source in...  92.1 us
    ppermute x42, starting transfers between devices, shifted(): lax.ppermute(value, axis, [(source, (source + step) % size) for source in...  76.4 us
    all_gather x1, waiting for transfers between devices, shards(): lax.all_gather(jnp.concatenate([key_rows, value_rows], axis=1), 'req', ax...  66.3 us
    ppermute x22, starting transfers between devices, swapped(): return lax.ppermute(value, axis, pairs)  46.7 us
    ppermute x22, waiting for transfers between devices, swapped(): return lax.ppermute(value, axis, pairs)  37.6 us
    unnamed x90, local copies, waits for them, and re-layouts  18.4 us
    while x4, local copies, waits for them, and re-layouts, fold_keys(): lax.scan(scan_step, running, (key_full, value_full, block_starts))  10.4 us
  transfers between devices with their start and end apart: 65, of which 46 were waited for; matrix products, arithmetic and copies ran while one was open for 5% of the time, Pallas kernels for 0%

profile of v2, /device:TPU:2, one launch (start us, length us, event | category | flops | bytes accessed | tf_op | source)
XLA Modules:
  0.0 436.1 jit_solution(237719418984212313)
XLA Ops:
  13.3 5.9 %collective-permute-start = (bf16[48,1536]{1,0:T(8,128)(2,1)S(1)}, bf16[48,1536]{1,0:T(8,128)(2,1)S(1)}, u32[]{:S(2)}, u32[]{:S(2)}) collective-permute-start(bf16[48,1536]{1,0:T(8,128)(2,1)S(1)} %get-tuple-element.242), channel_id=1, source_target_pairs={{0,7},{1,0},{2,1},{3,2},{4,3},{5,4},{6,5},{7,6},{8,15},{9,8},{10,9... | collective-permute-start | bytes 442376 | tf_op jit(solution)/shard_map/ppermute | solution.py:27
  19.1 4.3 copy.65
  23.5 3.3 collective-permute-start.1
  29.4 3.7 collective-permute-start.2
  33.8 5.7 %collective-permute-done.5 = bf16[48,1536]{1,0:T(8,128)(2,1)S(1)} collective-permute-done((bf16[48,1536]{1,0:T(8,128)(2,1)S(1)}, bf16[48,1536]{1,0:T(8,128)(2,1)S(1)}, u32[]{:S(2)}, u32[]{:S(2)}) %collective-permute-start.5) | collective-permute-done | bytes 147488 | tf_op jit(solution)/shard_map/ppermute | solution.py:27
  40.1 5.7 %collective-permute-done.6 = bf16[48,1536]{1,0:T(8,128)(2,1)S(1)} collective-permute-done((bf16[48,1536]{1,0:T(8,128)(2,1)S(1)}, bf16[48,1536]{1,0:T(8,128)(2,1)S(1)}, u32[]{:S(2)}, u32[]{:S(2)}) %collective-permute-start.6) | collective-permute-done | bytes 147488 | tf_op jit(solution)/shard_map/ppermute | solution.py:27
  60.3 2.8 collective-permute-start.11
  66.2 4.7 %collective-permute-start.12 = (f32[384]{0:T(512)S(1)}, f32[384]{0:T(512)S(1)}, u32[]{:S(2)}, u32[]{:S(2)}) collective-permute-start(f32[384]{0:T(512)S(1)} %add.441), channel_id=1, source_target_pairs={{0,4},{1,5},{2,6},{3,7},{4,0},{5,1},{6,2},{7,3},{8,12},{9,13},{10,... | collective-permute-start | bytes 4616 | tf_op jit(solution)/shard_map/ppermute | solution.py:22
  75.4 66.3 %all-gather.2.cloned.1.call-done = bf16[6144,512]{1,0:T(8,128)(2,1)} async-done(((bf16[384,512]{1,0:T(8,128)(2,1)}), bf16[6144,512]{1,0:T(8,128)(2,1)}) %all-gather.2.cloned.1.call-update) | async-done | bytes 6291472 | tf_op jit(solution)/shard_map/all_gather | solution.py:263
  141.7 5.9 %fusion.107 = (bf16[6144,256]{1,0:T(8,128)(2,1)}, bf16[6144,256]{1,0:T(8,128)(2,1)}) fusion(bf16[6144,512]{1,0:T(8,128)(2,1)} %all-gather.2.cloned.1.call-done), kind=kLoop, calls=%fused_computation.277 | loop fusion | bytes 12582912 | tf_op jit(solution)/shard_map/slice | solution.py:267
  147.6 4.7 %copy.66 = bf16[6,1024,256]{1,2,0:T(8,128)(2,1)} copy(bf16[6,1024,256]{2,1,0:T(8,128)(2,1)} %bitcast.247) | data formatting | bytes 6291456 | tf_op jit(solution)/shard_map/while | solution.py:158
  152.3 4.6 %copy.67 = bf16[6,1024,256]{1,2,0:T(8,128)(2,1)} copy(bf16[6,1024,256]{2,1,0:T(8,128)(2,1)} %bitcast.246) | data formatting | bytes 6291456 | tf_op jit(solution)/shard_map/while | solution.py:158
  156.9 25.6 %while.12 = (s32[]{:T(128)}, f32[384,256]{0,1:T(8,128)S(1)}, f32[384,2]{0,1:T(2,128)S(1)}, s32[6]{0:T(128)S(1)}, s32[3]{0:T(128)S(1)}, /*index=5*/pred[3]{0:T(51...) while((s32[]{:T(128)}, f32[384,256]{0,1:T(8,128)S(1)}, ...), condition=%wide.region_15.16_spmd, body=%wide.region_8.15_spmd.sunk | while | flops 407887872 | bytes 12441360 | solution.py:158
  160.0 3.6 conditional.2
  166.6 3.6 conditional.2
  189.1 2.5 collective-permute-start.14
  191.6 2.9 collective-permute-start.15
  196.6 3.1 collective-permute-start.17
  199.7 3.4 collective-permute-start.18
  203.1 3.4 collective-permute-done.14
  210.3 7.1 %collective-permute-start.30 = (f32[1536]{0:T(1024)S(1)}, f32[1536]{0:T(1024)S(1)}, u32[]{:S(2)}, u32[]{:S(2)}) collective-permute-start(f32[1536]{0:T(1024)S(1)} %reduce_sum.195), channel_id=1, source_target_pairs={{0,1},{1,0},{2,3},{3,2},{4,5},{5,4},{6,7},{7,6},{8,9},{9,8},{10,11... | collective-permute-start | bytes 18440 | tf_op jit(solution)/shard_map/ppermute | solution.py:22
  218.1 3.4 collective-permute-done.18
  225.1 2.6 collective-permute-start.20
  228.4 2.2 collective-permute-start.31
  231.8 2.9 collective-permute-start.21
  234.9 2.5 collective-permute-done.21
  237.4 3.7 collective-permute-start.22
  241.2 6.3 %collective-permute-done.25 = bf16[48,1536]{1,0:T(8,128)(2,1)S(1)} collective-permute-done((bf16[48,1536]{1,0:T(8,128)(2,1)S(1)}, bf16[48,1536]{1,0:T(8,128)(2,1)S(1)}, u32[]{:S(2)}, u32[]{:S(2)}) %collective-permute-start.25) | collective-permute-done | bytes 147488 | tf_op jit(solution)/shard_map/ppermute | solution.py:27
  247.6 6.3 %collective-permute-done.26 = bf16[48,1536]{1,0:T(8,128)(2,1)S(1)} collective-permute-done((bf16[48,1536]{1,0:T(8,128)(2,1)S(1)}, bf16[48,1536]{1,0:T(8,128)(2,1)S(1)}, u32[]{:S(2)}, u32[]{:S(2)}) %collective-permute-start.26) | collective-permute-done | bytes 147488 | tf_op jit(solution)/shard_map/ppermute | solution.py:27
  256.8 3.2 collective-permute-start.32
  261.8 2.9 reshape.297
  264.7 2.7 reshape_reshape_squeeze.3
  267.5 3.4 collective-permute-start.29
  270.8 4.4 %collective-permute-done.29 = f32[384]{0:T(512)S(1)} collective-permute-done((f32[384]{0:T(512)S(1)}, f32[384]{0:T(512)S(1)}, u32[]{:S(2)}, u32[]{:S(2)}) %collective-permute-start.29) | collective-permute-done | bytes 1568 | tf_op jit(solution)/shard_map/ppermute | solution.py:22
  275.2 3.4 fusion.116
  284.9 2.9 collective-permute-start.34
  289.5 2.9 collective-permute-start.36
  292.3 3.4 collective-permute-start.37
  297.0 4.4 %collective-permute-done.34 = bf16[48,1536]{1,0:T(8,128)(2,1)S(1)} collective-permute-done((bf16[48,1536]{1,0:T(8,128)(2,1)S(1)}, bf16[48,1536]{1,0:T(8,128)(2,1)S(1)}, u32[]{:S(2)}, u32[]{:S(2)}) %collective-permute-start.34) | collective-permute-done | bytes 147488 | tf_op jit(solution)/shard_map/ppermute | solution.py:27
  301.3 4.1 collective-permute-done.35
  306.5 5.0 %collective-permute-done.38 = bf16[48,1536]{1,0:T(8,128)(2,1)S(1)} collective-permute-done((bf16[48,1536]{1,0:T(8,128)(2,1)S(1)}, bf16[48,1536]{1,0:T(8,128)(2,1)S(1)}, u32[]{:S(2)}, u32[]{:S(2)}) %collective-permute-start.38) | collective-permute-done | bytes 147488 | tf_op jit(solution)/shard_map/ppermute | solution.py:27
  313.4 2.7 collective-permute-start.40
  316.7 2.2 collective-permute-done.40
  318.9 3.7 collective-permute-start.41
  322.8 2.4 collective-permute-done.41
  325.2 3.7 collective-permute-start.42
  329.2 7.6 %collective-permute-done.45 = bf16[48,1536]{1,0:T(8,128)(2,1)S(1)} collective-permute-done((bf16[48,1536]{1,0:T(8,128)(2,1)S(1)}, bf16[48,1536]{1,0:T(8,128)(2,1)S(1)}, u32[]{:S(2)}, u32[]{:S(2)}) %collective-permute-start.45) | collective-permute-done | bytes 147488 | tf_op jit(solution)/shard_map/ppermute | solution.py:27
  336.9 6.3 %collective-permute-done.46 = bf16[48,1536]{1,0:T(8,128)(2,1)S(1)} collective-permute-done((bf16[48,1536]{1,0:T(8,128)(2,1)S(1)}, bf16[48,1536]{1,0:T(8,128)(2,1)S(1)}, u32[]{:S(2)}, u32[]{:S(2)}) %collective-permute-start.46) | collective-permute-done | bytes 147488 | tf_op jit(solution)/shard_map/ppermute | solution.py:27
  343.5 2.2 fusion.32
  348.6 3.1 collective-permute-start.51
  351.7 3.0 collective-permute-start.52
  356.8 3.7 collective-permute-start.54
  360.4 5.3 %collective-permute-done.50 = bf16[48,1536]{1,0:T(8,128)(2,1)S(1)} collective-permute-done((bf16[48,1536]{1,0:T(8,128)(2,1)S(1)}, bf16[48,1536]{1,0:T(8,128)(2,1)S(1)}, u32[]{:S(2)}, u32[]{:S(2)}) %collective-permute-start.50) | collective-permute-done | bytes 147488 | tf_op jit(solution)/shard_map/ppermute | solution.py:27
  365.8 3.5 collective-permute-done.51
  371.1 3.6 collective-permute-done.54
  374.7 2.3 collective-permute-done.55
  380.3 3.3 collective-permute-done.57
  384.2 4.0 collective-permute-done.58
  388.4 3.0 collective-permute-start.59
  391.6 4.3 collective-permute-done.59
  396.0 14.6 %collective-permute-start.60 = (f32[9]{0:T(128)S(1)}, f32[9]{0:T(128)S(1)}, u32[]{:S(2)}, u32[]{:S(2)}) collective-permute-start(f32[9]{0:T(128)S(1)} %pad_maximum_fusion.8), channel_id=1, source_target_pairs={{0,8},{8,0},{16,24},{24,16},{32,40},{40,32},{48,56},{56,48},{64,72... | collective-permute-start | bytes 116 | tf_op jit(solution)/shard_map/ppermute | solution.py:22
  412.5 4.9 %collective-permute-done.61 = f32[9]{0:T(128)S(1)} collective-permute-done((f32[9]{0:T(128)S(1)}, f32[9]{0:T(128)S(1)}, u32[]{:S(2)}, u32[]{:S(2)}) %collective-permute-start.61) | collective-permute-done | bytes 68 | tf_op jit(solution)/shard_map/ppermute | solution.py:22
  417.8 3.4 collective-permute-done.62
  421.8 4.6 %collective-permute-done.63 = f32[9]{0:T(128)S(1)} collective-permute-done((f32[9]{0:T(128)S(1)}, f32[9]{0:T(128)S(1)}, u32[]{:S(2)}, u32[]{:S(2)}) %collective-permute-start.63) | collective-permute-done | bytes 68 | tf_op jit(solution)/shard_map/ppermute | solution.py:22
  (345 shorter events, 106.8 us)
Async XLA Ops:
  7.2 134.5 %all-gather.2.cloned.1.call-start = ((), (), s32[]{:S(2)}) async-start(), calls=%async_computation | async-start | bytes 6684672 | tf_op jit(solution)/shard_map/all_gather | solution.py:263
  13.3 10.2 %collective-permute-start = (bf16[48,1536]{1,0:T(8,128)(2,1)S(1)}, bf16[48,1536]{1,0:T(8,128)(2,1)S(1)}, u32[]{:S(2)}, u32[]{:S(2)}) collective-permute-start(bf16[48,1536]{1,0:T(8,128)(2,1)S(1)} %get-tuple-element.242), channel_id=1, source_target_pairs={{0,7},{1,0},{2,1},{3,2},{4,3},{5,4},{6,5},{7,6},{8,15},{9,8},{10,9... | collective-permute-start | bytes 442376 | tf_op jit(solution)/shard_map/ppermute | solution.py:27
  19.1 7.6 %collective-permute-start.3 = (bf16[48,1536]{1,0:T(8,128)(2,1)S(1)}, bf16[48,1536]{1,0:T(8,128)(2,1)S(1)}, u32[]{:S(2)}, u32[]{:S(2)}) collective-permute-start(bf16[48,1536]{1,0:T(8,128)(2,1)S(1)} %get-tuple-element.242), channel_id=1, source_target_pairs={{0,1},{1,2},{2,3},{3,4},{4,5},{5,6},{6,7},{7,0},{8,9},{9,10},{10,1... | collective-permute-start | bytes 442376 | tf_op jit(solution)/shard_map/ppermute | solution.py:27
  23.5 5.9 %collective-permute-start.1 = (bf16[48,1536]{1,0:T(8,128)(2,1)S(1)}, bf16[48,1536]{1,0:T(8,128)(2,1)S(1)}, u32[]{:S(2)}, u32[]{:S(2)}) collective-permute-start(bf16[48,1536]{1,0:T(8,128)(2,1)S(1)} %collective-permute-done), channel_id=1, source_target_pairs={{0,7},{1,0},{2,1},{3,2},{4,3},{5,4},{6,5},{7,6},{8,15},{9,8},{10,9... | collective-permute-start | bytes 442376 | tf_op jit(solution)/shard_map/ppermute | solution.py:27
  26.8 6.4 %collective-permute-start.4 = (bf16[48,1536]{1,0:T(8,128)(2,1)S(1)}, bf16[48,1536]{1,0:T(8,128)(2,1)S(1)}, u32[]{:S(2)}, u32[]{:S(2)}) collective-permute-start(bf16[48,1536]{1,0:T(8,128)(2,1)S(1)} %collective-permute-done.3), channel_id=1, source_target_pairs={{0,1},{1,2},{2,3},{3,4},{4,5},{5,6},{6,7},{7,0},{8,9},{9,10},{10,1... | collective-permute-start | bytes 442376 | tf_op jit(solution)/shard_map/ppermute | solution.py:27
  29.4 10.0 %collective-permute-start.2 = (bf16[48,1536]{1,0:T(8,128)(2,1)S(1)}, bf16[48,1536]{1,0:T(8,128)(2,1)S(1)}, u32[]{:S(2)}, u32[]{:S(2)}) collective-permute-start(bf16[48,1536]{1,0:T(8,128)(2,1)S(1)} %collective-permute-done.1), channel_id=1, source_target_pairs={{0,7},{1,0},{2,1},{3,2},{4,3},{5,4},{6,5},{7,6},{8,15},{9,8},{10,9... | collective-permute-start | bytes 442376 | tf_op jit(solution)/shard_map/ppermute | solution.py:27
  33.1 6.4 %collective-permute-start.5 = (bf16[48,1536]{1,0:T(8,128)(2,1)S(1)}, bf16[48,1536]{1,0:T(8,128)(2,1)S(1)}, u32[]{:S(2)}, u32[]{:S(2)}) collective-permute-start(bf16[48,1536]{1,0:T(8,128)(2,1)S(1)} %collective-permute-done.4), channel_id=1, source_target_pairs={{0,1},{1,2},{2,3},{3,4},{4,5},{5,6},{6,7},{7,0},{8,9},{9,10},{10,1... | collective-permute-start | bytes 442376 | tf_op jit(solution)/shard_map/ppermute | solution.py:27
  39.5 6.4 %collective-permute-start.6 = (bf16[48,1536]{1,0:T(8,128)(2,1)S(1)}, bf16[48,1536]{1,0:T(8,128)(2,1)S(1)}, u32[]{:S(2)}, u32[]{:S(2)}) collective-permute-start(bf16[48,1536]{1,0:T(8,128)(2,1)S(1)} %collective-permute-done.5), channel_id=1, source_target_pairs={{0,1},{1,2},{2,3},{3,4},{4,5},{5,6},{6,7},{7,0},{8,9},{9,10},{10,1... | collective-permute-start | bytes 442376 | tf_op jit(solution)/shard_map/ppermute | solution.py:27
  56.5 3.7 collective-permute-start.7
  56.6 3.7 collective-permute-start.10
  60.2 4.5 %collective-permute-start.8 = (f32[384]{0:T(512)S(1)}, f32[384]{0:T(512)S(1)}, u32[]{:S(2)}, u32[]{:S(2)}) collective-permute-start(f32[384]{0:T(512)S(1)} %add.436), channel_id=1, source_target_pairs={{0,2},{1,3},{2,0},{3,1},{4,6},{5,7},{6,4},{7,5},{8,10},{9,11},{10,... | collective-permute-start | bytes 4616 | tf_op jit(solution)/shard_map/ppermute | solution.py:22
  60.3 5.9 %collective-permute-start.11 = (f32[384]{0:T(512)S(1)}, f32[384]{0:T(512)S(1)}, u32[]{:S(2)}, u32[]{:S(2)}) collective-permute-start(f32[384]{0:T(512)S(1)} %add.440), channel_id=1, source_target_pairs={{0,2},{1,3},{2,0},{3,1},{4,6},{5,7},{6,4},{7,5},{8,10},{9,11},{10,... | collective-permute-start | bytes 4616 | tf_op jit(solution)/shard_map/ppermute | solution.py:22
  64.7 7.5 %collective-permute-start.9 = (f32[384]{0:T(512)S(1)}, f32[384]{0:T(512)S(1)}, u32[]{:S(2)}, u32[]{:S(2)}) collective-permute-start(f32[384]{0:T(512)S(1)} %add.437), channel_id=1, source_target_pairs={{0,4},{1,5},{2,6},{3,7},{4,0},{5,1},{6,2},{7,3},{8,12},{9,13},{10,... | collective-permute-start | bytes 4616 | tf_op jit(solution)/shard_map/ppermute | solution.py:22
  66.2 7.8 %collective-permute-start.12 = (f32[384]{0:T(512)S(1)}, f32[384]{0:T(512)S(1)}, u32[]{:S(2)}, u32[]{:S(2)}) collective-permute-start(f32[384]{0:T(512)S(1)} %add.441), channel_id=1, source_target_pairs={{0,4},{1,5},{2,6},{3,7},{4,0},{5,1},{6,2},{7,3},{8,12},{9,13},{10,... | collective-permute-start | bytes 4616 | tf_op jit(solution)/shard_map/ppermute | solution.py:22
  187.5 12.2 %collective-permute-start.13 = (bf16[48,1536]{1,0:T(8,128)(2,1)S(1)}, bf16[48,1536]{1,0:T(8,128)(2,1)S(1)}, u32[]{:S(2)}, u32[]{:S(2)}) collective-permute-start(bf16[48,1536]{1,0:T(8,128)(2,1)S(1)} %get-tuple-element.267), channel_id=1, source_target_pairs={{0,1},{1,2},{2,3},{3,4},{4,5},{5,6},{6,7},{7,0},{8,9},{9,10},{10,1... | collective-permute-start | bytes 442376 | tf_op jit(solution)/shard_map/ppermute | solution.py:27
  189.1 17.4 %collective-permute-start.14 = (bf16[48,1536]{1,0:T(8,128)(2,1)S(1)}, bf16[48,1536]{1,0:T(8,128)(2,1)S(1)}, u32[]{:S(2)}, u32[]{:S(2)}) collective-permute-start(bf16[48,1536]{1,0:T(8,128)(2,1)S(1)} %get-tuple-element.273), channel_id=1, source_target_pairs={{0,2},{1,3},{2,4},{3,5},{4,6},{5,7},{6,0},{7,1},{8,10},{9,11},{10,... | collective-permute-start | bytes 442376 | tf_op jit(solution)/shard_map/ppermute | solution.py:27
  191.6 18.7 %collective-permute-start.15 = (bf16[48,1536]{1,0:T(8,128)(2,1)}, bf16[48,1536]{1,0:T(8,128)(2,1)S(1)}, u32[]{:S(2)}, u32[]{:S(2)}) collective-permute-start(bf16[48,1536]{1,0:T(8,128)(2,1)} %get-tuple-element.272), channel_id=1, source_target_pairs={{0,3},{1,4},{2,5},{3,6},{4,7},{5,0},{6,1},{7,2},{8,11},{9,12},{10,... | collective-permute-start | bytes 442376 | tf_op jit(solution)/shard_map/ppermute | solution.py:27
  194.6 22.9 %collective-permute-start.16 = (bf16[48,1536]{1,0:T(8,128)(2,1)}, bf16[48,1536]{1,0:T(8,128)(2,1)}, u32[]{:S(2)}, u32[]{:S(2)}) collective-permute-start(bf16[48,1536]{1,0:T(8,128)(2,1)} %get-tuple-element.271), channel_id=1, source_target_pairs={{0,4},{1,5},{2,6},{3,7},{4,0},{5,1},{6,2},{7,3},{8,12},{9,13},{10,... | collective-permute-start | bytes 442376 | tf_op jit(solution)/shard_map/ppermute | solution.py:27
  196.6 21.5 %collective-permute-start.17 = (bf16[48,1536]{1,0:T(8,128)(2,1)}, bf16[48,1536]{1,0:T(8,128)(2,1)}, u32[]{:S(2)}, u32[]{:S(2)}) collective-permute-start(bf16[48,1536]{1,0:T(8,128)(2,1)} %get-tuple-element.270), channel_id=1, source_target_pairs={{0,5},{1,6},{2,7},{3,0},{4,1},{5,2},{6,3},{7,4},{8,13},{9,14},{10,... | collective-permute-start | bytes 442376 | tf_op jit(solution)/shard_map/ppermute | solution.py:27
  199.7 21.8 %collective-permute-start.18 = (bf16[48,1536]{1,0:T(8,128)(2,1)}, bf16[48,1536]{1,0:T(8,128)(2,1)}, u32[]{:S(2)}, u32[]{:S(2)}) collective-permute-start(bf16[48,1536]{1,0:T(8,128)(2,1)} %get-tuple-element.269), channel_id=1, source_target_pairs={{0,6},{1,7},{2,0},{3,1},{4,2},{5,3},{6,4},{7,5},{8,14},{9,15},{10,... | collective-permute-start | bytes 442376 | tf_op jit(solution)/shard_map/ppermute | solution.py:27
  206.5 16.8 %collective-permute-start.19 = (bf16[48,1536]{1,0:T(8,128)(2,1)S(1)}, bf16[48,1536]{1,0:T(8,128)(2,1)}, u32[]{:S(2)}, u32[]{:S(2)}) collective-permute-start(bf16[48,1536]{1,0:T(8,128)(2,1)S(1)} %get-tuple-element.268), channel_id=1, source_target_pairs={{0,7},{1,0},{2,1},{3,2},{4,3},{5,4},{6,5},{7,6},{8,15},{9,8},{10,9... | collective-permute-start | bytes 442376 | tf_op jit(solution)/shard_map/ppermute | solution.py:27
  210.3 18.0 %collective-permute-start.30 = (f32[1536]{0:T(1024)S(1)}, f32[1536]{0:T(1024)S(1)}, u32[]{:S(2)}, u32[]{:S(2)}) collective-permute-start(f32[1536]{0:T(1024)S(1)} %reduce_sum.195), channel_id=1, source_target_pairs={{0,1},{1,0},{2,3},{3,2},{4,5},{5,4},{6,7},{7,6},{8,9},{9,8},{10,11... | collective-permute-start | bytes 18440 | tf_op jit(solution)/shard_map/ppermute | solution.py:22
  225.1 6.7 %collective-permute-start.20 = (bf16[48,1536]{1,0:T(8,128)(2,1)S(1)}, bf16[48,1536]{1,0:T(8,128)(2,1)S(1)}, u32[]{:S(2)}, u32[]{:S(2)}) collective-permute-start(bf16[48,1536]{1,0:T(8,128)(2,1)S(1)} %get-tuple-element.238), channel_id=1, source_target_pairs={{0,7},{1,0},{2,1},{3,2},{4,3},{5,4},{6,5},{7,6},{8,15},{9,8},{10,9... | collective-permute-start | bytes 442376 | tf_op jit(solution)/shard_map/ppermute | solution.py:27
  227.8 7.1 %collective-permute-start.23 = (bf16[48,1536]{1,0:T(8,128)(2,1)S(1)}, bf16[48,1536]{1,0:T(8,128)(2,1)S(1)}, u32[]{:S(2)}, u32[]{:S(2)}) collective-permute-start(bf16[48,1536]{1,0:T(8,128)(2,1)S(1)} %get-tuple-element.238), channel_id=1, source_target_pairs={{0,1},{1,2},{2,3},{3,4},{4,5},{5,6},{6,7},{7,0},{8,9},{9,10},{10,1... | collective-permute-start | bytes 442376 | tf_op jit(solution)/shard_map/ppermute | solution.py:27
  228.4 28.4 %collective-permute-start.31 = (f32[1536]{0:T(1024)S(1)}, f32[1536]{0:T(1024)S(1)}, u32[]{:S(2)}, u32[]{:S(2)}) collective-permute-start(f32[1536]{0:T(1024)S(1)} %add.479), channel_id=1, source_target_pairs={{0,2},{1,3},{2,0},{3,1},{4,6},{5,7},{6,4},{7,5},{8,10},{9,11},{10,... | collective-permute-start | bytes 18440 | tf_op jit(solution)/shard_map/ppermute | solution.py:22
  231.8 5.6 %collective-permute-start.21 = (bf16[48,1536]{1,0:T(8,128)(2,1)S(1)}, bf16[48,1536]{1,0:T(8,128)(2,1)S(1)}, u32[]{:S(2)}, u32[]{:S(2)}) collective-permute-start(bf16[48,1536]{1,0:T(8,128)(2,1)S(1)} %collective-permute-done.20), channel_id=1, source_target_pairs={{0,7},{1,0},{2,1},{3,2},{4,3},{5,4},{6,5},{7,6},{8,15},{9,8},{10,9... | collective-permute-start | bytes 442376 | tf_op jit(solution)/shard_map/ppermute | solution.py:27
  234.8 6.4 %collective-permute-start.24 = (bf16[48,1536]{1,0:T(8,128)(2,1)S(1)}, bf16[48,1536]{1,0:T(8,128)(2,1)S(1)}, u32[]{:S(2)}, u32[]{:S(2)}) collective-permute-start(bf16[48,1536]{1,0:T(8,128)(2,1)S(1)} %collective-permute-done.23), channel_id=1, source_target_pairs={{0,1},{1,2},{2,3},{3,4},{4,5},{5,6},{6,7},{7,0},{8,9},{9,10},{10,1... | collective-permute-start | bytes 442376 | tf_op jit(solution)/shard_map/ppermute | solution.py:27
  237.4 10.1 %collective-permute-start.22 = (bf16[48,1536]{1,0:T(8,128)(2,1)S(1)}, bf16[48,1536]{1,0:T(8,128)(2,1)S(1)}, u32[]{:S(2)}, u32[]{:S(2)}) collective-permute-start(bf16[48,1536]{1,0:T(8,128)(2,1)S(1)} %collective-permute-done.21), channel_id=1, source_target_pairs={{0,7},{1,0},{2,1},{3,2},{4,3},{5,4},{6,5},{7,6},{8,15},{9,8},{10,9... | collective-permute-start | bytes 442376 | tf_op jit(solution)/shard_map/ppermute | solution.py:27
  241.2 6.4 %collective-permute-start.25 = (bf16[48,1536]{1,0:T(8,128)(2,1)S(1)}, bf16[48,1536]{1,0:T(8,128)(2,1)S(1)}, u32[]{:S(2)}, u32[]{:S(2)}) collective-permute-start(bf16[48,1536]{1,0:T(8,128)(2,1)S(1)} %collective-permute-done.24), channel_id=1, source_target_pairs={{0,1},{1,2},{2,3},{3,4},{4,5},{5,6},{6,7},{7,0},{8,9},{9,10},{10,1... | collective-permute-start | bytes 442376 | tf_op jit(solution)/shard_map/ppermute | solution.py:27
  247.6 6.4 %collective-permute-start.26 = (bf16[48,1536]{1,0:T(8,128)(2,1)S(1)}, bf16[48,1536]{1,0:T(8,128)(2,1)S(1)}, u32[]{:S(2)}, u32[]{:S(2)}) collective-permute-start(bf16[48,1536]{1,0:T(8,128)(2,1)S(1)} %collective-permute-done.25), channel_id=1, source_target_pairs={{0,1},{1,2},{2,3},{3,4},{4,5},{5,6},{6,7},{7,0},{8,9},{9,10},{10,1... | collective-permute-start | bytes 442376 | tf_op jit(solution)/shard_map/ppermute | solution.py:27
  256.3 3.6 collective-permute-start.27
  256.8 14.0 %collective-permute-start.32 = (f32[1536]{0:T(1024)S(1)}, f32[1536]{0:T(1024)S(1)}, u32[]{:S(2)}, u32[]{:S(2)}) collective-permute-start(f32[1536]{0:T(1024)S(1)} %add.480), channel_id=1, source_target_pairs={{0,4},{1,5},{2,6},{3,7},{4,0},{5,1},{6,2},{7,3},{8,12},{9,13},{10,... | collective-permute-start | bytes 18440 | tf_op jit(solution)/shard_map/ppermute | solution.py:22
  260.0 7.5 %collective-permute-start.28 = (f32[384]{0:T(512)S(1)}, f32[384]{0:T(512)S(1)}, u32[]{:S(2)}, u32[]{:S(2)}) collective-permute-start(f32[384]{0:T(512)S(1)} %add.475), channel_id=1, source_target_pairs={{0,2},{1,3},{2,0},{3,1},{4,6},{5,7},{6,4},{7,5},{8,10},{9,11},{10,... | collective-permute-start | bytes 4616 | tf_op jit(solution)/shard_map/ppermute | solution.py:22
  267.5 7.7 %collective-permute-start.29 = (f32[384]{0:T(512)S(1)}, f32[384]{0:T(512)S(1)}, u32[]{:S(2)}, u32[]{:S(2)}) collective-permute-start(f32[384]{0:T(512)S(1)} %add.476), channel_id=1, source_target_pairs={{0,4},{1,5},{2,6},{3,7},{4,0},{5,1},{6,2},{7,3},{8,12},{9,13},{10,... | collective-permute-start | bytes 4616 | tf_op jit(solution)/shard_map/ppermute | solution.py:22
  283.1 12.6 %collective-permute-start.33 = (bf16[48,1536]{1,0:T(8,128)(2,1)S(1)}, bf16[48,1536]{1,0:T(8,128)(2,1)S(1)}, u32[]{:S(2)}, u32[]{:S(2)}) collective-permute-start(bf16[48,1536]{1,0:T(8,128)(2,1)S(1)} %get-tuple-element.260), channel_id=1, source_target_pairs={{0,1},{1,2},{2,3},{3,4},{4,5},{5,6},{6,7},{7,0},{8,9},{9,10},{10,1... | collective-permute-start | bytes 442376 | tf_op jit(solution)/shard_map/ppermute | solution.py:27
  284.9 16.4 %collective-permute-start.34 = (bf16[48,1536]{1,0:T(8,128)(2,1)S(1)}, bf16[48,1536]{1,0:T(8,128)(2,1)S(1)}, u32[]{:S(2)}, u32[]{:S(2)}) collective-permute-start(bf16[48,1536]{1,0:T(8,128)(2,1)S(1)} %get-tuple-element.266), channel_id=1, source_target_pairs={{0,2},{1,3},{2,4},{3,5},{4,6},{5,7},{6,0},{7,1},{8,10},{9,11},{10,... | collective-permute-start | bytes 442376 | tf_op jit(solution)/shard_map/ppermute | solution.py:27
  287.9 17.5 %collective-permute-start.35 = (bf16[48,1536]{1,0:T(8,128)(2,1)S(1)}, bf16[48,1536]{1,0:T(8,128)(2,1)S(1)}, u32[]{:S(2)}, u32[]{:S(2)}) collective-permute-start(bf16[48,1536]{1,0:T(8,128)(2,1)S(1)} %get-tuple-element.265), channel_id=1, source_target_pairs={{0,3},{1,4},{2,5},{3,6},{4,7},{5,0},{6,1},{7,2},{8,11},{9,12},{10,... | collective-permute-start | bytes 442376 | tf_op jit(solution)/shard_map/ppermute | solution.py:27
  289.5 16.9 %collective-permute-start.36 = (bf16[48,1536]{1,0:T(8,128)(2,1)S(1)}, bf16[48,1536]{1,0:T(8,128)(2,1)S(1)}, u32[]{:S(2)}, u32[]{:S(2)}) collective-permute-start(bf16[48,1536]{1,0:T(8,128)(2,1)S(1)} %get-tuple-element.264), channel_id=1, source_target_pairs={{0,4},{1,5},{2,6},{3,7},{4,0},{5,1},{6,2},{7,3},{8,12},{9,13},{10,... | collective-permute-start | bytes 442376 | tf_op jit(solution)/shard_map/ppermute | solution.py:27
  292.3 14.2 %collective-permute-start.37 = (bf16[48,1536]{1,0:T(8,128)(2,1)S(1)}, bf16[48,1536]{1,0:T(8,128)(2,1)S(1)}, u32[]{:S(2)}, u32[]{:S(2)}) collective-permute-start(bf16[48,1536]{1,0:T(8,128)(2,1)S(1)} %get-tuple-element.263), channel_id=1, source_target_pairs={{0,5},{1,6},{2,7},{3,0},{4,1},{5,2},{6,3},{7,4},{8,13},{9,14},{10,... | collective-permute-start | bytes 442376 | tf_op jit(solution)/shard_map/ppermute | solution.py:27
  295.7 15.8 %collective-permute-start.38 = (bf16[48,1536]{1,0:T(8,128)(2,1)S(1)}, bf16[48,1536]{1,0:T(8,128)(2,1)S(1)}, u32[]{:S(2)}, u32[]{:S(2)}) collective-permute-start(bf16[48,1536]{1,0:T(8,128)(2,1)S(1)} %get-tuple-element.262), channel_id=1, source_target_pairs={{0,6},{1,7},{2,0},{3,1},{4,2},{5,3},{6,4},{7,5},{8,14},{9,15},{10,... | collective-permute-start | bytes 442376 | tf_op jit(solution)/shard_map/ppermute | solution.py:27
  301.3 11.5 %collective-permute-start.39 = (bf16[48,1536]{1,0:T(8,128)(2,1)S(1)}, bf16[48,1536]{1,0:T(8,128)(2,1)S(1)}, u32[]{:S(2)}, u32[]{:S(2)}) collective-permute-start(bf16[48,1536]{1,0:T(8,128)(2,1)S(1)} %get-tuple-element.261), channel_id=1, source_target_pairs={{0,7},{1,0},{2,1},{3,2},{4,3},{5,4},{6,5},{7,6},{8,15},{9,8},{10,9... | collective-permute-start | bytes 442376 | tf_op jit(solution)/shard_map/ppermute | solution.py:27
  313.4 5.4 %collective-permute-start.40 = (bf16[48,1536]{1,0:T(8,128)(2,1)S(1)}, bf16[48,1536]{1,0:T(8,128)(2,1)S(1)}, u32[]{:S(2)}, u32[]{:S(2)}) collective-permute-start(bf16[48,1536]{1,0:T(8,128)(2,1)S(1)} %get-tuple-element.234), channel_id=1, source_target_pairs={{0,7},{1,0},{2,1},{3,2},{4,3},{5,4},{6,5},{7,6},{8,15},{9,8},{10,9... | collective-permute-start | bytes 442376 | tf_op jit(solution)/shard_map/ppermute | solution.py:27
  316.2 6.4 %collective-permute-start.43 = (bf16[48,1536]{1,0:T(8,128)(2,1)S(1)}, bf16[48,1536]{1,0:T(8,128)(2,1)S(1)}, u32[]{:S(2)}, u32[]{:S(2)}) collective-permute-start(bf16[48,1536]{1,0:T(8,128)(2,1)S(1)} %get-tuple-element.234), channel_id=1, source_target_pairs={{0,1},{1,2},{2,3},{3,4},{4,5},{5,6},{6,7},{7,0},{8,9},{9,10},{10,1... | collective-permute-start | bytes 442376 | tf_op jit(solution)/shard_map/ppermute | solution.py:27
  316.2 27.3 %collective-permute-start.47 = (bf16[560,1536]{1,0:T(8,128)(2,1)S(1)}, bf16[560,1536]{1,0:T(8,128)(2,1)S(1)}, u32[]{:S(2)}, u32[]{:S(2)}) collective-permute-start(bf16[560,1536]{1,0:T(8,128)(2,1)S(1)} %copy-done.16), channel_id=1, source_target_pairs={{0,128},{128,0},{1,129},{129,1},{2,130},{130,2},{3,131},{131,3},{4... | collective-permute-start | bytes 5160968 | tf_op jit(solution)/shard_map/ppermute | solution.py:22
  316.2 30.7 %collective-permute-start.48 = (bf16[560,1536]{1,0:T(8,128)(2,1)S(1)}, bf16[560,1536]{1,0:T(8,128)(2,1)S(1)}, u32[]{:S(2)}, u32[]{:S(2)}) collective-permute-start(bf16[560,1536]{1,0:T(8,128)(2,1)S(1)} %copy-done.17), channel_id=1, source_target_pairs={{0,128},{128,0},{1,129},{129,1},{2,130},{130,2},{3,131},{131,3},{4... | collective-permute-start | bytes 5160968 | tf_op jit(solution)/shard_map/ppermute | solution.py:22
  318.9 6.4 %collective-permute-start.41 = (bf16[48,1536]{1,0:T(8,128)(2,1)S(1)}, bf16[48,1536]{1,0:T(8,128)(2,1)S(1)}, u32[]{:S(2)}, u32[]{:S(2)}) collective-permute-start(bf16[48,1536]{1,0:T(8,128)(2,1)S(1)} %collective-permute-done.40), channel_id=1, source_target_pairs={{0,7},{1,0},{2,1},{3,2},{4,3},{5,4},{6,5},{7,6},{8,15},{9,8},{10,9... | collective-permute-start | bytes 442376 | tf_op jit(solution)/shard_map/ppermute | solution.py:27
  322.5 6.7 %collective-permute-start.44 = (bf16[48,1536]{1,0:T(8,128)(2,1)S(1)}, bf16[48,1536]{1,0:T(8,128)(2,1)S(1)}, u32[]{:S(2)}, u32[]{:S(2)}) collective-permute-start(bf16[48,1536]{1,0:T(8,128)(2,1)S(1)} %collective-permute-done.43), channel_id=1, source_target_pairs={{0,1},{1,2},{2,3},{3,4},{4,5},{5,6},{6,7},{7,0},{8,9},{9,10},{10,1... | collective-permute-start | bytes 442376 | tf_op jit(solution)/shard_map/ppermute | solution.py:27
  325.2 11.6 %collective-permute-start.42 = (bf16[48,1536]{1,0:T(8,128)(2,1)S(1)}, bf16[48,1536]{1,0:T(8,128)(2,1)S(1)}, u32[]{:S(2)}, u32[]{:S(2)}) collective-permute-start(bf16[48,1536]{1,0:T(8,128)(2,1)S(1)} %collective-permute-done.41), channel_id=1, source_target_pairs={{0,7},{1,0},{2,1},{3,2},{4,3},{5,4},{6,5},{7,6},{8,15},{9,8},{10,9... | collective-permute-start | bytes 442376 | tf_op jit(solution)/shard_map/ppermute | solution.py:27
  329.2 7.6 %collective-permute-start.45 = (bf16[48,1536]{1,0:T(8,128)(2,1)S(1)}, bf16[48,1536]{1,0:T(8,128)(2,1)S(1)}, u32[]{:S(2)}, u32[]{:S(2)}) collective-permute-start(bf16[48,1536]{1,0:T(8,128)(2,1)S(1)} %collective-permute-done.44), channel_id=1, source_target_pairs={{0,1},{1,2},{2,3},{3,4},{4,5},{5,6},{6,7},{7,0},{8,9},{9,10},{10,1... | collective-permute-start | bytes 442376 | tf_op jit(solution)/shard_map/ppermute | solution.py:27
  336.9 6.4 %collective-permute-start.46 = (bf16[48,1536]{1,0:T(8,128)(2,1)S(1)}, bf16[48,1536]{1,0:T(8,128)(2,1)S(1)}, u32[]{:S(2)}, u32[]{:S(2)}) collective-permute-start(bf16[48,1536]{1,0:T(8,128)(2,1)S(1)} %collective-permute-done.45), channel_id=1, source_target_pairs={{0,1},{1,2},{2,3},{3,4},{4,5},{5,6},{6,7},{7,0},{8,9},{9,10},{10,1... | collective-permute-start | bytes 442376 | tf_op jit(solution)/shard_map/ppermute | solution.py:27
  348.2 8.6 %collective-permute-start.49 = (bf16[48,1536]{1,0:T(8,128)(2,1)S(1)}, bf16[48,1536]{1,0:T(8,128)(2,1)S(1)}, u32[]{:S(2)}, u32[]{:S(2)}) collective-permute-start(bf16[48,1536]{1,0:T(8,128)(2,1)S(1)} %get-tuple-element.253), channel_id=1, source_target_pairs={{0,1},{1,2},{2,3},{3,4},{4,5},{5,6},{6,7},{7,0},{8,9},{9,10},{10,1... | collective-permute-start | bytes 442376 | tf_op jit(solution)/shard_map/ppermute | solution.py:27
  348.3 17.5 %collective-permute-start.50 = (bf16[48,1536]{1,0:T(8,128)(2,1)S(1)}, bf16[48,1536]{1,0:T(8,128)(2,1)S(1)}, u32[]{:S(2)}, u32[]{:S(2)}) collective-permute-start(bf16[48,1536]{1,0:T(8,128)(2,1)S(1)} %get-tuple-element.259), channel_id=1, source_target_pairs={{0,2},{1,3},{2,4},{3,5},{4,6},{5,7},{6,0},{7,1},{8,10},{9,11},{10,... | collective-permute-start | bytes 442376 | tf_op jit(solution)/shard_map/ppermute | solution.py:27
  348.6 20.7 %collective-permute-start.51 = (bf16[48,1536]{1,0:T(8,128)(2,1)S(1)}, bf16[48,1536]{1,0:T(8,128)(2,1)S(1)}, u32[]{:S(2)}, u32[]{:S(2)}) collective-permute-start(bf16[48,1536]{1,0:T(8,128)(2,1)S(1)} %get-tuple-element.258), channel_id=1, source_target_pairs={{0,3},{1,4},{2,5},{3,6},{4,7},{5,0},{6,1},{7,2},{8,11},{9,12},{10,... | collective-permute-start | bytes 442376 | tf_op jit(solution)/shard_map/ppermute | solution.py:27
  351.7 17.8 %collective-permute-start.52 = (bf16[48,1536]{1,0:T(8,128)(2,1)S(1)}, bf16[48,1536]{1,0:T(8,128)(2,1)S(1)}, u32[]{:S(2)}, u32[]{:S(2)}) collective-permute-start(bf16[48,1536]{1,0:T(8,128)(2,1)S(1)} %get-tuple-element.257), channel_id=1, source_target_pairs={{0,4},{1,5},{2,6},{3,7},{4,0},{5,1},{6,2},{7,3},{8,12},{9,13},{10,... | collective-permute-start | bytes 442376 | tf_op jit(solution)/shard_map/ppermute | solution.py:27
  354.8 16.3 %collective-permute-start.53 = (bf16[48,1536]{1,0:T(8,128)(2,1)S(1)}, bf16[48,1536]{1,0:T(8,128)(2,1)S(1)}, u32[]{:S(2)}, u32[]{:S(2)}) collective-permute-start(bf16[48,1536]{1,0:T(8,128)(2,1)S(1)} %get-tuple-element.256), channel_id=1, source_target_pairs={{0,5},{1,6},{2,7},{3,0},{4,1},{5,2},{6,3},{7,4},{8,13},{9,14},{10,... | collective-permute-start | bytes 442376 | tf_op jit(solution)/shard_map/ppermute | solution.py:27
  356.8 17.9 %collective-permute-start.54 = (bf16[48,1536]{1,0:T(8,128)(2,1)S(1)}, bf16[48,1536]{1,0:T(8,128)(2,1)S(1)}, u32[]{:S(2)}, u32[]{:S(2)}) collective-permute-start(bf16[48,1536]{1,0:T(8,128)(2,1)S(1)} %get-tuple-element.255), channel_id=1, source_target_pairs={{0,6},{1,7},{2,0},{3,1},{4,2},{5,3},{6,4},{7,5},{8,14},{9,15},{10,... | collective-permute-start | bytes 442376 | tf_op jit(solution)/shard_map/ppermute | solution.py:27
  365.8 11.3 %collective-permute-start.55 = (bf16[48,1536]{1,0:T(8,128)(2,1)S(1)}, bf16[48,1536]{1,0:T(8,128)(2,1)S(1)}, u32[]{:S(2)}, u32[]{:S(2)}) collective-permute-start(bf16[48,1536]{1,0:T(8,128)(2,1)S(1)} %get-tuple-element.254), channel_id=1, source_target_pairs={{0,7},{1,0},{2,1},{3,2},{4,3},{5,4},{6,5},{7,6},{8,15},{9,8},{10,9... | collective-permute-start | bytes 442376 | tf_op jit(solution)/shard_map/ppermute | solution.py:27
  380.0 3.6 collective-permute-start.57
  383.7 4.5 %collective-permute-start.58 = (f32[9]{0:T(128)S(1)}, f32[9]{0:T(128)S(1)}, u32[]{:S(2)}, u32[]{:S(2)}) collective-permute-start(f32[9]{0:T(128)S(1)} %pad_maximum_fusion.6), channel_id=1, source_target_pairs={{0,2},{1,3},{2,0},{3,1},{4,6},{5,7},{6,4},{7,5},{8,10},{9,11},{10,... | collective-permute-start | bytes 116 | tf_op jit(solution)/shard_map/ppermute | solution.py:22
  388.4 7.5 %collective-permute-start.59 = (f32[9]{0:T(128)S(1)}, f32[9]{0:T(128)S(1)}, u32[]{:S(2)}, u32[]{:S(2)}) collective-permute-start(f32[9]{0:T(128)S(1)} %pad_maximum_fusion.7), channel_id=1, source_target_pairs={{0,4},{1,5},{2,6},{3,7},{4,0},{5,1},{6,2},{7,3},{8,12},{9,13},{10,... | collective-permute-start | bytes 116 | tf_op jit(solution)/shard_map/ppermute | solution.py:22
  396.0 16.1 %collective-permute-start.60 = (f32[9]{0:T(128)S(1)}, f32[9]{0:T(128)S(1)}, u32[]{:S(2)}, u32[]{:S(2)}) collective-permute-start(f32[9]{0:T(128)S(1)} %pad_maximum_fusion.8), channel_id=1, source_target_pairs={{0,8},{8,0},{16,24},{24,16},{32,40},{40,32},{48,56},{56,48},{64,72... | collective-permute-start | bytes 116 | tf_op jit(solution)/shard_map/ppermute | solution.py:22
  412.3 5.1 %collective-permute-start.61 = (f32[9]{0:T(128)S(1)}, f32[9]{0:T(128)S(1)}, u32[]{:S(2)}, u32[]{:S(2)}) collective-permute-start(f32[9]{0:T(128)S(1)} %pad_maximum_fusion.9), channel_id=1, source_target_pairs={{0,16},{8,24},{16,0},{24,8},{32,48},{40,56},{48,32},{56,40},{64,80... | collective-permute-start | bytes 116 | tf_op jit(solution)/shard_map/ppermute | solution.py:22
  417.6 3.6 collective-permute-start.62
  421.3 5.1 %collective-permute-start.63 = (f32[9]{0:T(128)S(1)}, f32[9]{0:T(128)S(1)}, u32[]{:S(2)}, u32[]{:S(2)}) collective-permute-start(f32[9]{0:T(128)S(1)} %pad_maximum_fusion.11), channel_id=1, source_target_pairs={{0,64},{8,72},{16,80},{24,88},{32,96},{40,104},{48,112},{56,120},{... | collective-permute-start | bytes 116 | tf_op jit(solution)/shard_map/ppermute | solution.py:22
  (23 other events, 683.7 us)
Sparse Core Ops, SparseCore 0:
  75.1 66.4 all-gather.1
